TPU v7x, 128 devices: a whole 4x4x4 slice. The times are simulated.
128 devices in a mesh: seq: 16 (over x, z_hi, core), tp: 8 (over z_lo, y).
Axes of the slice: x: 4, y: 4, z: 4 (z_hi: 2, z_lo: 2; z = z_hi * 2 + z_lo), core: 2. Of those that a mesh axis runs over, the one named last changes fastest.
Arguments:
- tokens: bfloat16 [4096, 5120], P('seq', 'tp'), may hold values from -6 to 6
- norm_gain: float32 [5120], replicated, may hold values from 0.1 to 1.9
- q_weight: bfloat16 [5120, 5120], P(None, 'tp'), may hold values from -0.078125 to 0.078125
- kv_weight: bfloat16 [5120, 2, 1024], P(None, None, 'tp'), may hold values from -0.078125 to 0.078125
- out_weight: bfloat16 [5120, 5120], P('tp'), may hold values from -0.5 to 0.5
- ctx_cache: bfloat16 [16384, 2, 1024], P('seq', None, 'tp'), may hold values from -1000 to 1000, as said below
- span_start: int32 [1], replicated, may hold values from 4096 to 16384
- finished_cache: bfloat16 [4, 16384, 2, 1024], P(None, 'seq', None, 'tp'), may hold values from -6 to 6
- block_dest: int32 [1024, 1], P('seq'), may hold values from 0 to 15; in each aligned block of 64 rows (0 to 63, 64 to 127, ...) at most 8 rows name the same one
Outputs:
- attended: bfloat16 [4096, 5120], P('seq', 'tp')
- page_pool: bfloat16 [4, 32768, 2, 1024], P(None, 'seq', None, 'tp')
Inputs may be any that keep to these rules, and one draw needn't show every extreme that they name: `block_dest`: among the 64 blocks of one index of seq, no decode index is named more than 8 times, and some decode index is named exactly 8 times. `ctx_cache`: keys are stored already rotated at their positions; keys may reach some hundreds in magnitude, values lie within -6 to 6.
All inputs are finite; a program needn't handle non-finite values.
Results may differ from a plain program's by a relative error of at most 0.03.
The roundings to bfloat16 on the way count: a program that leaves them out, or rounds other values in their place, can miss the bound.
Values may be sent and summed in bfloat16 or wider, within the bound.
No kernel may reach another device: no remote copies, remote signals or barrier semaphores. Data moves between devices by JAX's collectives and lax.ppermute only.
A program may use at most 128 MiB of HBM per device.

v0:
```python
import math

import jax
import jax.numpy as jnp
from jax import lax
from jax.sharding import PartitionSpec as P

D = 5120
HD = 128
LAYERS = 4
BLK = 16


rms_eps = 1e-06
rope_base = 1000000.0
neg_fill = -1e30


def rotate_pairs(values, positions):
    half_width = values.shape[-1] // 2
    frequency = jnp.exp(
        jnp.arange(half_width, dtype=jnp.float32) * (-2.0 * math.log(rope_base) / values.shape[-1])
    )
    angles = positions[:, None] * frequency[None, :]
    cosine = jnp.cos(angles)[:, None, :]
    sine_part = jnp.sin(angles)[:, None, :]
    first_half = values[..., :half_width]
    second_half = values[..., half_width:]
    return jnp.concatenate(
        [
            first_half * cosine - second_half * sine_part,
            second_half * cosine + first_half * sine_part,
        ],
        -1,
    )


def attend(running, queries, query_first, key_rows, key_first, span_first, cached_rows, span_rows):
    row_count = key_rows.shape[0]
    kv_heads = queries.shape[1]
    query_count = queries.shape[0]
    cycle_rows = cached_rows + span_rows
    global_rows = key_first + jnp.arange(row_count, dtype=jnp.int32)
    shard_index = global_rows // cycle_rows
    offset = global_rows % cycle_rows
    in_cache = offset < cached_rows
    cache_place = shard_index * cached_rows + offset
    span_place = shard_index * span_rows + offset - cached_rows
    query_place = query_first + jnp.arange(query_count, dtype=jnp.int32)
    visible = jnp.where(
        in_cache[None, :],
        (cache_place < span_first)[None, :],
        span_place[None, :] <= query_place[:, None],
    )
    row_max, row_total, summed = running
    head_keys = key_rows[:, 0].reshape(row_count, kv_heads, HD)
    head_values = key_rows[:, 1].reshape(row_count, kv_heads, HD)
    scores = jnp.einsum(
        "tkgd,skd->tkgs", queries, head_keys, preferred_element_type=jnp.float32
    ) * HD ** (-0.5)
    visible_mask = visible[:, None, None, :]
    new_max = jnp.maximum(row_max, jnp.max(jnp.where(visible_mask, scores, neg_fill), -1))
    weights = jnp.where(visible_mask, jnp.exp(scores - new_max[..., None]), 0.0)
    rescale = jnp.exp(row_max - new_max)
    new_total = row_total * rescale + jnp.sum(weights, -1)
    new_summed = summed * rescale[..., None] + jnp.einsum(
        "tkgs,skd->tkgd",
        weights.astype(jnp.bfloat16),
        head_values,
        preferred_element_type=jnp.float32,
    )
    return (new_max, new_total, new_summed)


def fold_blocks(running, queries, query_first, key_rows, span_first, cached_rows, span_rows):
    piece_rows = key_rows.shape[0]
    unit_rows = cached_rows + span_rows
    block_count = piece_rows // unit_rows
    stacked = key_rows.reshape((block_count, unit_rows) + key_rows.shape[1:])

    def scan_step(current, inputs_pair):
        key_block, block_index = inputs_pair
        return (
            attend(
                current,
                queries,
                query_first,
                key_block,
                block_index * unit_rows,
                span_first,
                cached_rows,
                span_rows,
            ),
            None,
        )

    final_state, ignored = lax.scan(
        scan_step, running, (stacked, jnp.arange(block_count, dtype=jnp.int32))
    )
    return final_state


def on_device(
    tokens,
    norm_gain,
    q_weight,
    kv_weight,
    out_weight,
    ctx_cache,
    span_start,
    finished_cache,
    block_dest,
):
    seq_count = lax.axis_size("seq")
    seq_place = lax.axis_index("seq")
    tok_rows = tokens.shape[0]
    cached_rows = ctx_cache.shape[0]
    kv_heads = kv_weight.shape[2] // HD
    head_group = q_weight.shape[1] // HD // kv_heads
    kv_width = kv_heads * HD
    gathered = lax.all_gather(tokens, "tp", axis=1, tiled=True)
    widened = gathered.astype(jnp.float32)
    normed = (
        widened
        * lax.rsqrt(jnp.mean(widened * widened, axis=-1, keepdims=True) + rms_eps)
        * norm_gain
    ).astype(jnp.bfloat16)
    span_first = span_start[0]
    positions = (span_first + seq_place * tok_rows + jnp.arange(tok_rows, dtype=jnp.int32)).astype(
        jnp.float32
    )
    queries = jnp.dot(normed, q_weight, preferred_element_type=jnp.float32).reshape(
        tok_rows, kv_heads * head_group, HD
    )
    queries = (
        rotate_pairs(queries, positions)
        .astype(jnp.bfloat16)
        .reshape(tok_rows, kv_heads, head_group, HD)
    )
    projected = jnp.dot(
        normed, kv_weight.reshape(D, 2 * kv_width), preferred_element_type=jnp.float32
    ).reshape(tok_rows, 2, kv_heads, HD)
    new_keys = (
        rotate_pairs(projected[:, 0], positions).astype(jnp.bfloat16).reshape(tok_rows, kv_width)
    )
    new_values = projected[:, 1].astype(jnp.bfloat16).reshape(tok_rows, kv_width)
    local_rows = jnp.concatenate([ctx_cache, jnp.stack([new_keys, new_values], 1)], 0)
    empty_state = (
        jnp.full((tok_rows, kv_heads, head_group), neg_fill, jnp.float32),
        jnp.zeros((tok_rows, kv_heads, head_group), jnp.float32),
        jnp.zeros((tok_rows, kv_heads, head_group, HD), jnp.float32),
    )
    row_max, row_total, summed = fold_blocks(
        empty_state,
        queries,
        seq_place * tok_rows,
        lax.all_gather(local_rows, "seq", axis=0, tiled=True),
        span_first,
        cached_rows,
        tok_rows,
    )
    mixed_heads = (
        (summed / row_total[..., None])
        .astype(jnp.bfloat16)
        .reshape(tok_rows, kv_width * head_group)
    )
    reduced = lax.psum_scatter(
        lax.dot_general(
            out_weight, mixed_heads, (((0,), (1,)), ((), ())), preferred_element_type=jnp.float32
        ).astype(jnp.bfloat16),
        "tp",
        scatter_dimension=0,
        tiled=True,
    ).astype(jnp.float32)
    attended = reduced.T.astype(jnp.bfloat16)
    block_total = block_dest.shape[0]
    capacity = 2 * block_total // seq_count
    destination = block_dest[:, 0]
    onehot = (destination[:, None] == jnp.arange(seq_count, dtype=jnp.int32)[None, :]).astype(
        jnp.int32
    )
    earlier_count = jnp.sum((jnp.cumsum(onehot, axis=0, dtype=jnp.int32) - onehot) * onehot, axis=1)
    slot_index = destination * capacity + earlier_count
    slot_match = slot_index[None, :] == jnp.arange(seq_count * capacity, dtype=jnp.int32)[:, None]
    filled = jnp.any(slot_match, axis=1)
    source_block = jnp.sum(
        jnp.where(slot_match, jnp.arange(block_total, dtype=jnp.int32)[None, :], 0), axis=1
    )
    blocks = finished_cache.reshape(LAYERS, block_total, BLK, 2, kv_width)
    outgoing = jnp.where(
        filled[None, :, None, None, None],
        jnp.take(blocks, source_block, axis=1),
        jnp.zeros((), blocks.dtype),
    )
    outgoing = outgoing.reshape(LAYERS, seq_count, capacity * BLK, 2, kv_width)
    incoming = lax.all_to_all(outgoing, "seq", split_axis=1, concat_axis=1, tiled=True)
    page_pool = incoming.reshape(LAYERS, seq_count * capacity * BLK, 2, kv_width)
    return (attended, page_pool)


def solution(mesh):
    return jax.shard_map(
        on_device,
        mesh=mesh,
        in_specs=(
            P("seq", "tp"),
            P(),
            P(None, "tp"),
            P(None, None, "tp"),
            P("tp", None),
            P("seq", None, "tp"),
            P(),
            P(None, "seq", None, "tp"),
            P("seq", None),
        ),
        out_specs=(P("seq", "tp"), P(None, "seq", None, "tp")),
        check_vma=False,
    )
```

profile of v0, /device:TPU:1, one launch (start us, length us, event | category | flops | bytes accessed | tf_op | source)
XLA Modules:
  0.0 507.4 jit_solution(313747012844102346)
XLA Ops:
  8.6 2.1 copy.104
  10.7 2.8 copy.80
  14.6 37.1 %all-gather.3.cloned.1.call-done = bf16[256,5120]{1,0:T(8,128)(2,1)} async-done(((bf16[256,640]{1,0:T(8,128)(2,1)}), bf16[256,5120]{1,0:T(8,128)(2,1)}) %all-gather.3.cloned.1.call-update) | async-done | bytes 2621456 | tf_op jit(solution)/shard_map/all_gather | solution.py:121
  51.7 2.3 fusion.27
  54.1 3.7 fusion.31
  60.0 5.7 %fusion.33 = f32[256,640]{0,1:T(8,128)S(1)} fusion(bf16[5120,640]{1,0:T(8,128)(2,1)} %param.13, bf16[256,5120]{1,0:T(8,128)(2,1)S(1)} %copy-done.1, f32[5120]{0:T(1024)S(1)} %copy-done.3, f32[256]{0:T(256)S(1)} %add_rsqrt_fusion), kind=kOutput, calls=%fused_computation.52 | convolution fusion | flops 1682964480 | bytes 9851904 | tf_op jit(solution)/shard_map/dot_general | solution.py:132
  66.0 78.2 %all-gather.5.cloned.1.call-done = bf16[20480,2,128]{2,0,1:T(8,128)(2,1)} async-done(((bf16[1280,2,128]{2,0,1:T(8,128)(2,1)}), bf16[20480,2,128]{2,0,1:T(8,128)(2,1)}) %all-gather.5.cloned.1.call-update) | async-done | bytes 10485776 | tf_op jit(solution)/shard_map/all_gather | solution.py:157
  144.2 227.4 %while.17 = (s32[]{:T(128)}, f32[256,1,5]{0,2,1:T(8,128)S(1)}, f32[256,1,5]{0,2,1:T(8,128)S(1)}, f32[256,1,5,128]{0,3,2,1:T(8,128)S(1)}, s32[16]{0:T(128)S(1)}, ...) while((s32[]{:T(128)}, f32[256,1,5]{0,2,1:T(8,128)S(1)}, ...), condition=%wide.region_4.5_spmd.clone, body=%wide.region_1.4_spmd.clone.sunk | while | flops 858080256 | bytes 50896072 | solution.py:97
  148.3 3.9 fusion.60
  152.2 4.6 fusion.63
  157.0 1.4 fusion.62
  162.5 3.9 fusion.60
  166.4 4.6 fusion.63
  171.2 1.4 fusion.62
  176.8 3.9 fusion.60
  180.7 4.6 fusion.63
  185.4 1.4 fusion.62
  191.0 3.9 fusion.60
  194.9 4.6 fusion.63
  199.6 1.4 fusion.62
  205.2 3.9 fusion.60
  209.1 4.6 fusion.63
  213.8 1.4 fusion.62
  219.4 3.9 fusion.60
  223.3 4.6 fusion.63
  228.0 1.4 fusion.62
  233.6 3.9 fusion.60
  237.5 4.6 fusion.63
  242.3 1.4 fusion.62
  247.8 3.9 fusion.60
  251.7 4.6 fusion.63
  256.5 1.4 fusion.62
  262.0 3.9 fusion.60
  266.0 4.6 fusion.63
  270.7 1.4 fusion.62
  276.3 3.9 fusion.60
  280.2 4.6 fusion.63
  284.9 1.4 fusion.62
  290.5 3.9 fusion.60
  294.4 4.6 fusion.63
  299.1 1.4 fusion.62
  304.7 3.9 fusion.60
  308.6 4.6 fusion.63
  318.9 3.9 fusion.60
  322.8 4.6 fusion.63
  333.1 3.9 fusion.60
  337.0 4.6 fusion.63
  341.8 1.4 fusion.62
  347.3 3.9 fusion.60
  351.2 4.6 fusion.63
  356.0 1.4 fusion.62
  361.6 3.9 fusion.60
  365.5 4.6 fusion.63
  370.2 1.4 fusion.62
  371.7 5.1 %fusion.26 = bf16[5120,256]{0,1:T(8,128)(2,1)S(1)} fusion(bf16[256,640]{0,1:T(8,128)(2,1)S(1)} %bitcast.149, bf16[640,5120]{1,0:T(8,128)(2,1)} %param.15), kind=kOutput, calls=%fused_computation.43 | convolution fusion | flops 1679032320 | bytes 9502720 | tf_op jit(solution)/shard_map/dot_general | solution.py:168
  376.8 2.6 copy.99
  379.4 1.9 copy.88
  381.6 3.1 gather_fusion
  384.7 5.1 %copy.89 = bf16[4,128,16,2,128]{4,2,1,3,0:T(8,128)(2,1)} copy(bf16[4,128,16,2,128]{4,2,3,0,1:T(8,128)(2,1)} %bitcast.140) | data formatting | bytes 8388608 | tf_op jit(solution)/shard_map/jit(_take)/gather | solution.py:192
  390.4 4.0 fusion.30
  394.4 6.6 %copy.90 = bf16[4,16,128,2,128]{4,3,2,0,1:T(2,128)(2,1)S(1)} copy(bf16[4,16,128,2,128]{4,2,1,3,0:T(8,128)(2,1)} %fusion.30) | data formatting | bytes 8388608 | tf_op jit(solution)/shard_map/jit(_where)/select_n | solution.py:190
  401.0 61.4 %all_to_all.5 = bf16[4,16,128,2,128]{4,3,2,0,1:T(2,128)(2,1)S(1)} all-to-all(bf16[4,16,128,2,128]{4,3,2,0,1:T(2,128)(2,1)S(1)} %copy.90), channel_id=1, replica_groups=mesh['seq'=16,'tp'=8] {'seq'}, dimensions={1} | all-to-all | bytes 8388608 | tf_op jit(solution)/shard_map/all_to_all | solution.py:196
  463.5 35.4 %copy.92 = bf16[4,2048,2,128]{3,2,1,0:T(2,128)(2,1)} copy(bf16[4,2048,2,128]{3,1,2,0:T(8,128)(2,1)S(1)} %bitcast.141) | data formatting | bytes 8388608
  499.0 1.9 copy.100
  (226 shorter events, 66.6 us)
Async XLA Ops:
  7.2 44.5 %all-gather.3.cloned.1.call-start = ((), (), s32[]{:S(2)}) async-start(), calls=%async_computation.2 | async-start | bytes 2949120 | tf_op jit(solution)/shard_map/all_gather | solution.py:121
  7.9 136.3 %all-gather.5.cloned.1.call-start = ((), (), s32[]{:S(2)}) async-start(), calls=%async_computation.3 | async-start | bytes 11141120 | tf_op jit(solution)/shard_map/all_gather | solution.py:157
  10.7 43.4 %copy-start.3 = (f32[5120]{0:T(1024)S(1)}, f32[5120]{0:T(1024)}, u32[]{:S(2)}) copy-start(f32[5120]{0:T(1024)} %param.12) | copy-start | bytes 61444
  54.0 5.2 %copy-start.2 = (s32[64,1]{0,1:T(1,128)S(1)}, s32[64,1]{0,1:T(1,128)}, u32[]{:S(2)}) copy-start(s32[64,1]{0,1:T(1,128)} %param.19) | copy-start | bytes 772
  54.0 5.9 %copy-start.1 = (bf16[256,5120]{1,0:T(8,128)(2,1)S(1)}, bf16[256,5120]{1,0:T(8,128)(2,1)}, u32[]{:S(2)}) copy-start(bf16[256,5120]{1,0:T(8,128)(2,1)} %all-gather.3.cloned.1.call-done) | copy-start | bytes 7864324
  59.2 439.8 %reduce-scatter.4.cloned.1.call-start = ((), (), s32[]{:S(2)}) async-start(), calls=%async_computation.4 | async-start | bytes 2949120
  152.2 4.7 copy-start
  166.4 4.7 copy-start
  180.7 4.7 copy-start
  194.9 4.7 copy-start
  209.1 4.7 copy-start
  223.3 4.7 copy-start
  237.5 4.7 copy-start
  251.7 4.7 copy-start
  265.9 4.7 copy-start
  280.2 4.7 copy-start
  294.4 4.7 copy-start
  308.6 4.7 copy-start
  322.8 4.7 copy-start
  337.0 4.7 copy-start
  351.2 4.7 copy-start
  365.5 4.7 copy-start
Sparse Core Ops, SparseCore 0:
  9.6 42.0 all-gather.2
  59.3 84.8 all-gather.4
  379.5 43.9 reduce-scatter.3
where the time goes:
time: 509 us; the launch traced here: 507 us
  matrix products  151 us (30%)
  waiting for transfers between devices  116 us (23%)
  local copies, waits for them, and re-layouts  94 us (18%)
  blocking collectives  61.4 us (12%)
  other arithmetic  58.8 us (12%)
  between operations  14.7 us (3%)
  loops' own time  11.6 us (2%)
    all_gather x1, waiting for transfers between devices, on_device(): lax.all_gather(local_rows, 'seq', axis=0, tiled=True)  78.2 us
    dot_general x16, matrix products, attend(): jnp.einsum('tkgs,skd->tkgd', weights.astype(jnp.bfloat16), head_values, p...  74 us
    dot_general x16, matrix products, attend(): jnp.einsum('tkgd,skd->tkgs', queries, head_keys, preferred_element_type=j...  62.3 us
    all_to_all x1, blocking collectives, on_device(): lax.all_to_all(outgoing, 'seq', split_axis=1, concat_axis=1, tiled=True)  61.4 us
    unnamed x12, local copies, waits for them, and re-layouts  43.3 us
    all_gather x1, waiting for transfers between devices, on_device(): gathered = lax.all_gather(tokens, 'tp', axis=1, tiled=True)  37.1 us
    reduce_sum x16, other arithmetic, attend(): new_total = row_total * rescale + jnp.sum(weights, -1)  22 us
    squeeze x16, local copies, waits for them, and re-layouts, fold_blocks(): lax.scan(scan_step, running, (stacked, jnp.arange(block_count, dtype=jnp....  18.3 us
  transfers between devices with their start and end apart: 3, of which 2 were waited for; matrix products, arithmetic and copies ran while one was open for 14% of the time, Pallas kernels for 0%

commit v1 on v0

v1 whole, which is shorter than its diff:
```python
import math
import functools

import jax
import jax.numpy as jnp
from jax import lax
from jax.experimental import pallas as pl
from jax.experimental.pallas import tpu as pltpu
from jax.sharding import PartitionSpec as P

D = 5120
HD = 128
LAYERS = 4
BLK = 16
CTX_BLOCK = 1024


rms_eps = 1e-06
rope_base = 1000000.0
neg_fill = -1e30


def rotate_pairs(values, positions):
    half_width = values.shape[-1] // 2
    frequency = jnp.exp(
        jnp.arange(half_width, dtype=jnp.float32) * (-2.0 * math.log(rope_base) / values.shape[-1])
    )
    angles = positions[:, None] * frequency[None, :]
    cosine = jnp.cos(angles)[:, None, :]
    sine_part = jnp.sin(angles)[:, None, :]
    first_half = values[..., :half_width]
    second_half = values[..., half_width:]
    return jnp.concatenate(
        [
            first_half * cosine - second_half * sine_part,
            second_half * cosine + first_half * sine_part,
        ],
        -1,
    )


def flash_kernel(
    scalars, q_ref, kv_ref, m_in, l_in, acc_in, m_ref, l_ref, acc_ref,
    *, block_rows, tok_rows, causal
):
    step = pl.program_id(0)
    span_first = scalars[0]
    seq_place = scalars[1]

    @pl.when(step == 0)
    def _():
        m_ref[...] = m_in[...]
        l_ref[...] = l_in[...]
        acc_ref[...] = acc_in[...]

    if causal:
        live = step <= seq_place
    else:
        live = step * block_rows < span_first

    @pl.when(live)
    def _():
        q = q_ref[...]
        k = kv_ref[:, :HD]
        v = kv_ref[:, HD:]
        scores = lax.dot_general(
            q, k, (((1,), (1,)), ((), ())), preferred_element_type=jnp.float32
        ) * HD ** (-0.5)
        col = lax.broadcasted_iota(jnp.int32, scores.shape, 1) + step * block_rows
        if causal:
            row = (lax.broadcasted_iota(jnp.int32, scores.shape, 0) & (tok_rows - 1)) + seq_place * tok_rows
            visible = col <= row
        else:
            visible = col < span_first
        row_max = m_ref[...]
        new_max = jnp.maximum(row_max, jnp.max(jnp.where(visible, scores, neg_fill), 1, keepdims=True))
        weights = jnp.where(visible, jnp.exp(scores - new_max), 0.0)
        rescale = jnp.exp(row_max - new_max)
        l_ref[...] = l_ref[...] * rescale + jnp.sum(weights, 1, keepdims=True)
        acc_ref[...] = acc_ref[...] * rescale + jnp.dot(
            weights.astype(jnp.bfloat16), v, preferred_element_type=jnp.float32
        )
        m_ref[...] = new_max


def flash_pass(scalars, queries, kv_rows, state, block_rows, tok_rows, causal):
    rows = queries.shape[0]
    block_count = kv_rows.shape[0] // block_rows
    if causal:
        def kv_map(j, s):
            return (jnp.minimum(j, s[1]), 0)
    else:
        def kv_map(j, s):
            last = (s[0] + block_rows - 1) // block_rows - 1
            return (jnp.maximum(jnp.minimum(j, last), 0), 0)
    full = lambda j, s: (0, 0)
    kernel = functools.partial(
        flash_kernel, block_rows=block_rows, tok_rows=tok_rows, causal=causal
    )
    return pl.pallas_call(
        kernel,
        out_shape=(
            jax.ShapeDtypeStruct((rows, 1), jnp.float32),
            jax.ShapeDtypeStruct((rows, 1), jnp.float32),
            jax.ShapeDtypeStruct((rows, HD), jnp.float32),
        ),
        grid_spec=pltpu.PrefetchScalarGridSpec(
            num_scalar_prefetch=1,
            grid=(block_count,),
            in_specs=[
                pl.BlockSpec((rows, HD), full),
                pl.BlockSpec((block_rows, 2 * HD), kv_map),
                pl.BlockSpec((rows, 1), full),
                pl.BlockSpec((rows, 1), full),
                pl.BlockSpec((rows, HD), full),
            ],
            out_specs=[
                pl.BlockSpec((rows, 1), full),
                pl.BlockSpec((rows, 1), full),
                pl.BlockSpec((rows, HD), full),
            ],
        ),
        compiler_params=pltpu.CompilerParams(
            dimension_semantics=("arbitrary",), vmem_limit_bytes=48 * 1024 * 1024
        ),
    )(scalars, queries, kv_rows, *state)


def on_device(
    tokens,
    norm_gain,
    q_weight,
    kv_weight,
    out_weight,
    ctx_cache,
    span_start,
    finished_cache,
    block_dest,
):
    seq_count = lax.axis_size("seq")
    seq_place = lax.axis_index("seq")
    tok_rows = tokens.shape[0]
    kv_heads = kv_weight.shape[2] // HD
    head_group = q_weight.shape[1] // HD // kv_heads
    kv_width = kv_heads * HD
    ctx_rows = ctx_cache.reshape(ctx_cache.shape[0], 2 * kv_width)
    ctx_all = lax.all_gather(ctx_rows, "seq", axis=0, tiled=True)
    gathered = lax.all_gather(tokens, "tp", axis=1, tiled=True)
    widened = gathered.astype(jnp.float32)
    normed = (
        widened
        * lax.rsqrt(jnp.mean(widened * widened, axis=-1, keepdims=True) + rms_eps)
        * norm_gain
    ).astype(jnp.bfloat16)
    span_first = span_start[0]
    positions = (span_first + seq_place * tok_rows + jnp.arange(tok_rows, dtype=jnp.int32)).astype(
        jnp.float32
    )
    queries = jnp.dot(normed, q_weight, preferred_element_type=jnp.float32).reshape(
        tok_rows, kv_heads * head_group, HD
    )
    queries = rotate_pairs(queries, positions).astype(jnp.bfloat16)
    queries = jnp.transpose(queries, (1, 0, 2)).reshape(head_group * tok_rows, HD)
    projected = jnp.dot(
        normed, kv_weight.reshape(D, 2 * kv_width), preferred_element_type=jnp.float32
    ).reshape(tok_rows, 2, kv_heads, HD)
    new_keys = (
        rotate_pairs(projected[:, 0], positions).astype(jnp.bfloat16).reshape(tok_rows, kv_width)
    )
    new_values = projected[:, 1].astype(jnp.bfloat16).reshape(tok_rows, kv_width)
    new_rows = jnp.concatenate([new_keys, new_values], 1)
    new_all = lax.all_gather(new_rows, "seq", axis=0, tiled=True)
    query_rows = head_group * tok_rows
    scalars = jnp.stack([span_first, seq_place]).astype(jnp.int32)
    empty_state = (
        jnp.full((query_rows, 1), neg_fill, jnp.float32),
        jnp.zeros((query_rows, 1), jnp.float32),
        jnp.zeros((query_rows, HD), jnp.float32),
    )
    state = flash_pass(scalars, queries, ctx_all, empty_state, CTX_BLOCK, tok_rows, False)
    row_max, row_total, summed = flash_pass(scalars, queries, new_all, state, tok_rows, tok_rows, True)
    mixed_heads = (
        (summed / row_total)
        .astype(jnp.bfloat16)
        .reshape(head_group, tok_rows, HD)
    )
    mixed_heads = jnp.transpose(mixed_heads, (1, 0, 2)).reshape(tok_rows, kv_width * head_group)
    reduced = lax.psum_scatter(
        lax.dot_general(
            out_weight, mixed_heads, (((0,), (1,)), ((), ())), preferred_element_type=jnp.float32
        ).astype(jnp.bfloat16),
        "tp",
        scatter_dimension=0,
        tiled=True,
    ).astype(jnp.float32)
    attended = reduced.T.astype(jnp.bfloat16)
    block_total = block_dest.shape[0]
    capacity = 2 * block_total // seq_count
    destination = block_dest[:, 0]
    onehot = (destination[:, None] == jnp.arange(seq_count, dtype=jnp.int32)[None, :]).astype(
        jnp.int32
    )
    earlier_count = jnp.sum((jnp.cumsum(onehot, axis=0, dtype=jnp.int32) - onehot) * onehot, axis=1)
    slot_index = destination * capacity + earlier_count
    slot_match = slot_index[None, :] == jnp.arange(seq_count * capacity, dtype=jnp.int32)[:, None]
    filled = jnp.any(slot_match, axis=1)
    source_block = jnp.sum(
        jnp.where(slot_match, jnp.arange(block_total, dtype=jnp.int32)[None, :], 0), axis=1
    )
    blocks = finished_cache.reshape(LAYERS, block_total, BLK, 2, kv_width)
    outgoing = jnp.where(
        filled[None, :, None, None, None],
        jnp.take(blocks, source_block, axis=1),
        jnp.zeros((), blocks.dtype),
    )
    outgoing = outgoing.reshape(LAYERS, seq_count, capacity * BLK, 2, kv_width)
    incoming = lax.all_to_all(outgoing, "seq", split_axis=1, concat_axis=1, tiled=True)
    page_pool = incoming.reshape(LAYERS, seq_count * capacity * BLK, 2, kv_width)
    return (attended, page_pool)


def solution(mesh):
    return jax.shard_map(
        on_device,
        mesh=mesh,
        in_specs=(
            P("seq", "tp"),
            P(),
            P(None, "tp"),
            P(None, None, "tp"),
            P("tp", None),
            P("seq", None, "tp"),
            P(),
            P(None, "seq", None, "tp"),
            P("seq", None),
        ),
        out_specs=(P("seq", "tp"), P(None, "seq", None, "tp")),
        check_vma=False,
    )
```

time: 509 us -> 375 us (0.74)
  matrix products: 151 us -> 14.5 us
  blocking collectives: 61.4 us -> 112 us
  other arithmetic: 58.8 us -> 8.75 us
  Pallas kernels: 0 us -> 49.7 us
  local copies, waits for them, and re-layouts: 94 us -> 64.3 us
  loops' own time: 11.6 us -> 0 us
  waiting for transfers between devices: 116 us -> 110 us
    dot_general x32 -> x0, matrix products: 136 us -> none  [the longest x16 74 us: attend(): jnp.einsum('tkgs,skd->tkgd', weights.astype(jnp.bfloat16), head_values, p...]
    all_to_all x1, blocking collectives: 61.4 us -> 112 us  [on_device(): lax.all_to_all(outgoing, 'seq', split_axis=1, concat_axis=1, tiled=True)]
    pallas_call x0 -> x2, Pallas kernels: none -> 49.7 us  [flash_pass(): pl.pallas_call(kernel, out_shape=(jax.ShapeDtypeStruct((rows, 1), jnp.flo...]
    reduce_sum x16 -> x0, other arithmetic: 22 us -> none  [attend(): new_total = row_total * rescale + jnp.sum(weights, -1)]
    squeeze x16 -> x0, local copies, waits for them, and re-layouts: 18.3 us -> none  [fold_blocks(): lax.scan(scan_step, running, (stacked, jnp.arange(block_count, dtype=jnp....]
    select_n x16 -> x0, other arithmetic: 16.7 us -> none  [attend(): jnp.where(in_cache[None, :], (cache_place < span_first)[None, :], span_pl...]
    another operation x1 -> x0, loops' own time: 11.6 us -> none  [fold_blocks(): lax.scan(scan_step, running, (stacked, jnp.arange(block_count, dtype=jnp....]
    lt x16 -> x0, other arithmetic: 10.7 us -> none  [attend(): cache_place < span_first]
  transfers between devices with their start and end apart: 3 -> 4, of which waited for: 2 -> 3; matrix products, arithmetic and copies ran while one was open for 14% -> 20% of each run, Pallas kernels for 0% -> 11%
where the time goes in v1:
time: 375 us; the launch traced here: 374 us
  blocking collectives  112 us (30%)
  waiting for transfers between devices  110 us (29%)
  local copies, waits for them, and re-layouts  64.3 us (17%)
  Pallas kernels  49.7 us (13%)
  between operations  14.7 us (4%)
  matrix products  14.5 us (4%)
  other arithmetic  8.75 us (2%)
    all_to_all x1, blocking collectives, on_device(): lax.all_to_all(outgoing, 'seq', split_axis=1, concat_axis=1, tiled=True)  112 us
    all_gather x1, waiting for transfers between devices, on_device(): ctx_all = lax.all_gather(ctx_rows, 'seq', axis=0, tiled=True)  64.5 us
    pallas_call x2, Pallas kernels, flash_pass(): pl.pallas_call(kernel, out_shape=(jax.ShapeDtypeStruct((rows, 1), jnp.flo...  49.7 us
    unnamed x13, local copies, waits for them, and re-layouts  44.8 us
    all_gather x1, waiting for transfers between devices, on_device(): gathered = lax.all_gather(tokens, 'tp', axis=1, tiled=True)  36.2 us
    all_gather x1, waiting for transfers between devices, on_device(): new_all = lax.all_gather(new_rows, 'seq', axis=0, tiled=True)  8.43 us
  transfers between devices with their start and end apart: 4, of which 3 were waited for; matrix products, arithmetic and copies ran while one was open for 20% of the time, Pallas kernels for 11%

profile of v1, /device:TPU:1, one launch (start us, length us, event | category | flops | bytes accessed | tf_op | source)
XLA Modules:
  0.0 374.0 jit_solution(4282667358987884639)
XLA Ops:
  7.2 0.0 all-gather.4.cloned.1.call-start
  7.2 0.7 all-gather.4.cloned.1.call-update
  7.9 0.0 all-gather.8.cloned.1.call-start
  7.9 2.0 copy.77
  9.9 0.0 all-gather.8.cloned.1.call-update
  9.9 0.0 all-gather.6.cloned.1.call-start
  10.6 2.1 copy.76
  12.7 0.0 copy-start.3
  12.7 2.8 copy.57
  15.5 36.2 %all-gather.4.cloned.1.call-done = bf16[256,5120]{1,0:T(8,128)(2,1)} async-done(((bf16[256,640]{1,0:T(8,128)(2,1)}), bf16[256,5120]{1,0:T(8,128)(2,1)}) %all-gather.4.cloned.1.call-update) | async-done | bytes 2621456 | tf_op jit(solution)/shard_map/all_gather | solution.py:148
  51.7 2.3 fusion.1
  54.0 0.0 copy-done.3
  54.0 0.0 copy-start.2
  54.0 0.0 copy-start.1
  54.1 3.6 fusion.7
  57.7 0.6 fusion.23
  58.3 0.8 pad_maximum_fusion
  59.1 0.0 all-gather.6.cloned.1.call-update
  59.1 0.0 reduce-scatter.4.cloned.1.call-start
  59.1 0.0 copy-done.2
  59.1 0.1 fusion.25
  59.2 0.1 reduce_window_sum.11
  59.3 0.1 pad_add_fusion.scalars
  59.4 0.2 select_reduce_fusion.1
  59.6 0.3 multiply_cosine_fusion.1
  59.9 0.0 copy-done.1
  59.9 5.8 %fusion.11 = f32[256,640]{0,1:T(8,128)S(1)} fusion(bf16[5120,640]{1,0:T(8,128)(2,1)} %param.11, bf16[256,5120]{1,0:T(8,128)(2,1)S(1)} %copy-done.1, f32[5120]{0:T(1024)S(1)} %copy-done.3, f32[256]{0:T(256)S(1)} %add_rsqrt_fusion), kind=kOutput, calls=%fused_computation.14 | convolution fusion | flops 1682964480 | bytes 9851904 | tf_op jit(solution)/shard_map/dot_general | solution.py:159
  65.7 0.1 subtract_convert_fusion
  65.8 0.2 copy.56
  66.0 64.5 %all-gather.8.cloned.1.call-done.kv_ref = bf16[16384,256]{1,0:T(8,128)(2,1)} async-done(((bf16[1024,256]{1,0:T(8,128)(2,1)}), bf16[16384,256]{1,0:T(8,128)(2,1)}) %all-gather.8.cloned.1.call-update) | async-done | bytes 8388624 | tf_op jit(solution)/shard_map/all_gather | solution.py:147
  130.6 40.2 %shard_map.104 = (f32[1280,1]{1,0:T(8,128)S(1)}, f32[1280,1]{1,0:T(8,128)S(1)}, f32[1280,128]{1,0:T(8,128)S(1)}) custom-call(s32[2]{0:T(128)S(1)} %pad_add_fusion.scalars, bf16[1280,128]{1,0:T(8,128)(2,1)S(1)} %bitcast.60, bf16[16384,256]{1,0:T(8,128)(2,1)} %all-gather.8.cloned.1.call-done.kv_ref, f32[1280,1]{1,0:T(8,128)S(1)} %broadcast_in_dim.68.m_in, ...), custom_call_target="tpu_custom_call" | custom-call | tf_op jit(solution)/shard_map/pallas_call | solution.py:100
  170.9 8.4 %all-gather.6.cloned.1.call-done.kv_ref = bf16[4096,256]{1,0:T(8,128)(2,1)} async-done(((bf16[256,256]{1,0:T(8,128)(2,1)}), bf16[4096,256]{1,0:T(8,128)(2,1)}) %all-gather.6.cloned.1.call-update) | async-done | bytes 2097168 | tf_op jit(solution)/shard_map/all_gather | solution.py:172
  179.3 9.5 %shard_map.105 = (f32[1280,1]{1,0:T(8,128)}, f32[1280,1]{1,0:T(8,128)S(1)}, f32[1280,128]{1,0:T(8,128)S(1)}) custom-call(s32[2]{0:T(128)S(1)} %pad_add_fusion.scalars, bf16[1280,128]{1,0:T(8,128)(2,1)S(1)} %bitcast.61, bf16[4096,256]{1,0:T(8,128)(2,1)} %all-gather.6.cloned.1.call-done.kv_ref, f32[1280,1]{1,0:T(8,128)S(1)} %get-tuple-element.7.m_in, ...), custom_call_target="tpu_custom_call" | custom-call | tf_op jit(solution)/shard_map/pallas_call | solution.py:100
  188.7 0.0 copy-start
  188.7 0.8 copy-done
  189.6 0.2 reduce
  189.8 1.3 divide_convert_fusion
  191.2 0.2 copy.59
  191.3 5.1 %fusion = bf16[5120,256]{0,1:T(8,128)(2,1)S(1)} fusion(bf16[256,640]{0,1:T(8,128)(2,1)S(1)} %bitcast.70, bf16[640,5120]{1,0:T(8,128)(2,1)} %param.13), kind=kOutput, calls=%fused_computation.4 | convolution fusion | flops 1679032320 | bytes 9502720 | tf_op jit(solution)/shard_map/dot_general | solution.py:189
  196.4 2.6 copy.70
  199.0 0.0 reduce-scatter.4.cloned.1.call-update
  199.1 0.1 select_reduce_fusion
  199.2 0.1 reduce_sum.34
  199.3 0.1 broadcast_in_dim.77
  199.4 0.1 broadcast_in_dim.78
  199.4 0.1 fusion.24
  199.5 0.1 broadcast_in_dim.71
  199.6 0.1 broadcast_in_dim.72
  199.7 0.1 broadcast_in_dim.73
  199.8 1.9 copy.61
  201.8 3.1 gather_fusion
  204.9 2.9 copy.62
  207.9 2.4 fusion.4
  210.3 6.6 %copy.63 = bf16[4,16,128,2,128]{4,3,2,0,1:T(2,128)(2,1)S(1)} copy(bf16[4,16,128,2,128]{4,2,1,3,0:T(8,128)(2,1)} %fusion.4) | data formatting | bytes 8388608 | tf_op jit(solution)/shard_map/jit(_where)/select_n | solution.py:211
  216.9 112.1 %all_to_all.5 = bf16[4,16,128,2,128]{4,3,2,0,1:T(2,128)(2,1)S(1)} all-to-all(bf16[4,16,128,2,128]{4,3,2,0,1:T(2,128)(2,1)S(1)} %copy.63), channel_id=1, replica_groups=mesh['seq'=16,'tp'=8] {'seq'}, dimensions={1} | all-to-all | bytes 8388608 | tf_op jit(solution)/shard_map/all_to_all | solution.py:217
  329.0 1.1 copy.64
  330.1 35.4 %copy.65 = bf16[4,2048,2,128]{3,2,1,0:T(2,128)(2,1)} copy(bf16[4,2048,2,128]{3,1,2,0:T(8,128)(2,1)S(1)} %bitcast.63) | data formatting | bytes 8388608
  365.6 0.0 reduce-scatter.4.cloned.1.call-done
  365.6 1.9 copy.71
  (13 shorter events, 0.2 us)
Async XLA Ops:
  7.2 44.5 %all-gather.4.cloned.1.call-start = ((), (), s32[]{:S(2)}) async-start(), calls=%async_computation.2 | async-start | bytes 2949120 | tf_op jit(solution)/shard_map/all_gather | solution.py:148
  7.9 122.6 %all-gather.8.cloned.1.call-start = ((), (), s32[]{:S(2)}) async-start(), calls=%async_computation.4 | async-start | bytes 8912896 | tf_op jit(solution)/shard_map/all_gather | solution.py:147
  9.9 169.4 %all-gather.6.cloned.1.call-start = ((), (), s32[]{:S(2)}) async-start(), calls=%async_computation.3 | async-start | bytes 2228224 | tf_op jit(solution)/shard_map/all_gather | solution.py:172
  12.7 41.3 %copy-start.3 = (f32[5120]{0:T(1024)S(1)}, f32[5120]{0:T(1024)}, u32[]{:S(2)}) copy-start(f32[5120]{0:T(1024)} %param.10) | copy-start | bytes 61444
  54.0 5.1 %copy-start.2 = (s32[64,1]{0,1:T(1,128)S(1)}, s32[64,1]{0,1:T(1,128)}, u32[]{:S(2)}) copy-start(s32[64,1]{0,1:T(1,128)} %param.17) | copy-start | bytes 772
  54.0 5.8 %copy-start.1 = (bf16[256,5120]{1,0:T(8,128)(2,1)S(1)}, bf16[256,5120]{1,0:T(8,128)(2,1)}, u32[]{:S(2)}) copy-start(bf16[256,5120]{1,0:T(8,128)(2,1)} %all-gather.4.cloned.1.call-done) | copy-start | bytes 7864324
  59.1 306.5 %reduce-scatter.4.cloned.1.call-start = ((), (), s32[]{:S(2)}) async-start(), calls=%async_computation.5 | async-start | bytes 2949120
  188.7 0.8 copy-start
Sparse Core Ops, SparseCore 0:
  9.6 42.0 all-gather.3
  54.1 76.3 all-gather.7
  133.5 45.7 all-gather.5
  199.2 94.1 reduce-scatter.3

commit v2 on v1

--- a/solution.py
+++ b/solution.py
@@ -126,6 +126,40 @@
     )(scalars, queries, kv_rows, *state)
 
 
+def move_pages(finished_cache, block_dest, seq_count, seq_place, kv_width):
+    block_total = block_dest.shape[0]
+    capacity = 2 * block_total // seq_count
+    destination = (block_dest[:, 0] - seq_place) % seq_count
+    onehot = (destination[:, None] == jnp.arange(seq_count, dtype=jnp.int32)[None, :]).astype(
+        jnp.int32
+    )
+    earlier_count = jnp.sum((jnp.cumsum(onehot, axis=0, dtype=jnp.int32) - onehot) * onehot, axis=1)
+    slot_index = destination * capacity + earlier_count
+    slot_match = slot_index[None, :] == jnp.arange(seq_count * capacity, dtype=jnp.int32)[:, None]
+    filled = jnp.any(slot_match, axis=1)
+    source_block = jnp.sum(
+        jnp.where(slot_match, jnp.arange(block_total, dtype=jnp.int32)[None, :], 0), axis=1
+    )
+    blocks = finished_cache.reshape(LAYERS, block_total, BLK, 2, kv_width)
+    outgoing = jnp.where(
+        filled[None, :, None, None, None],
+        jnp.take(blocks, source_block, axis=1),
+        jnp.zeros((), blocks.dtype),
+    )
+    outgoing = outgoing.reshape(LAYERS, seq_count, capacity * BLK, 2, kv_width)
+    piece_rows = capacity * BLK
+    page_pool = jnp.zeros((LAYERS, seq_count * piece_rows, 2, kv_width), blocks.dtype)
+    for shift in range(seq_count):
+        piece = outgoing[:, shift]
+        if shift:
+            piece = lax.ppermute(
+                piece, "seq", [(s, (s + shift) % seq_count) for s in range(seq_count)]
+            )
+        source = (seq_place - shift) % seq_count
+        page_pool = lax.dynamic_update_slice(page_pool, piece, (0, source * piece_rows, 0, 0))
+    return page_pool
+
+
 def on_device(
     tokens,
     norm_gain,
@@ -145,6 +179,8 @@
     kv_width = kv_heads * HD
     ctx_rows = ctx_cache.reshape(ctx_cache.shape[0], 2 * kv_width)
     ctx_all = lax.all_gather(ctx_rows, "seq", axis=0, tiled=True)
+    page_pool = move_pages(finished_cache, block_dest, seq_count, seq_place, kv_width)
+    page_pool, ctx_all = lax.optimization_barrier((page_pool, ctx_all))
     gathered = lax.all_gather(tokens, "tp", axis=1, tiled=True)
     widened = gathered.astype(jnp.float32)
     normed = (
@@ -194,28 +230,6 @@
         tiled=True,
     ).astype(jnp.float32)
     attended = reduced.T.astype(jnp.bfloat16)
-    block_total = block_dest.shape[0]
-    capacity = 2 * block_total // seq_count
-    destination = block_dest[:, 0]
-    onehot = (destination[:, None] == jnp.arange(seq_count, dtype=jnp.int32)[None, :]).astype(
-        jnp.int32
-    )
-    earlier_count = jnp.sum((jnp.cumsum(onehot, axis=0, dtype=jnp.int32) - onehot) * onehot, axis=1)
-    slot_index = destination * capacity + earlier_count
-    slot_match = slot_index[None, :] == jnp.arange(seq_count * capacity, dtype=jnp.int32)[:, None]
-    filled = jnp.any(slot_match, axis=1)
-    source_block = jnp.sum(
-        jnp.where(slot_match, jnp.arange(block_total, dtype=jnp.int32)[None, :], 0), axis=1
-    )
-    blocks = finished_cache.reshape(LAYERS, block_total, BLK, 2, kv_width)
-    outgoing = jnp.where(
-        filled[None, :, None, None, None],
-        jnp.take(blocks, source_block, axis=1),
-        jnp.zeros((), blocks.dtype),
-    )
-    outgoing = outgoing.reshape(LAYERS, seq_count, capacity * BLK, 2, kv_width)
-    incoming = lax.all_to_all(outgoing, "seq", split_axis=1, concat_axis=1, tiled=True)
-    page_pool = incoming.reshape(LAYERS, seq_count * capacity * BLK, 2, kv_width)
     return (attended, page_pool)
 
 

time: 375 us -> 330 us (0.88); the launches traced: 374 us -> 325 us
  blocking collectives: 112 us -> 0 us
  waiting for transfers between devices: 110 us -> 173 us
  starting transfers between devices: 0.16 us -> 33 us
  Pallas kernels: 49.7 us -> 32.6 us
  local copies, waits for them, and re-layouts: 64.3 us -> 48.5 us
    all_to_all x1 -> x0, blocking collectives: 112 us -> none  [on_device(): lax.all_to_all(outgoing, 'seq', split_axis=1, concat_axis=1, tiled=True)]
    unnamed x5, waiting for transfers between devices: 0.73 us -> 85.2 us
    all_gather x1, waiting for transfers between devices: 64.5 us -> 10.8 us  [on_device(): ctx_all = lax.all_gather(ctx_rows, 'seq', axis=0, tiled=True)]
    ppermute x0 -> x15, waiting for transfers between devices: none -> 46.5 us  [move_pages(): lax.ppermute(piece, 'seq', [(s, (s + shift) % seq_count) for s in range(s...]
    all_gather x1, waiting for transfers between devices: 36.2 us -> 0.01 us  [on_device(): gathered = lax.all_gather(tokens, 'tp', axis=1, tiled=True)]
    unnamed x13 -> x12, local copies, waits for them, and re-layouts: 44.8 us -> 11.1 us
    ppermute x0 -> x15, starting transfers between devices: none -> 32.8 us  [move_pages(): lax.ppermute(piece, 'seq', [(s, (s + shift) % seq_count) for s in range(s...]
    all_gather x1, waiting for transfers between devices: 8.43 us -> 30.7 us  [on_device(): new_all = lax.all_gather(new_rows, 'seq', axis=0, tiled=True)]
  transfers between devices with their start and end apart: 4 -> 19, of which waited for: 3 -> 10; matrix products, arithmetic and copies ran while one was open for 20% -> 18% of each run, Pallas kernels for 11% -> 7%
where the time goes in v2:
time: 330 us; the launch traced here: 325 us
  waiting for transfers between devices  173 us (52%)
  local copies, waits for them, and re-layouts  48.5 us (15%)
  starting transfers between devices  33 us (10%)
  Pallas kernels  32.6 us (10%)
  between operations  14.7 us (4%)
  matrix products  14.4 us (4%)
  other arithmetic  8.48 us (3%)
    unnamed x5, waiting for transfers between devices  85.2 us
    ppermute x15, waiting for transfers between devices, move_pages(): lax.ppermute(piece, 'seq', [(s, (s + shift) % seq_count) for s in range(s...  46.5 us
    ppermute x15, starting transfers between devices, move_pages(): lax.ppermute(piece, 'seq', [(s, (s + shift) % seq_count) for s in range(s...  32.8 us
    pallas_call x2, Pallas kernels, flash_pass(): pl.pallas_call(kernel, out_shape=(jax.ShapeDtypeStruct((rows, 1), jnp.flo...  32.6 us
    all_gather x1, waiting for transfers between devices, on_device(): new_all = lax.all_gather(new_rows, 'seq', axis=0, tiled=True)  30.7 us
    dynamic_update_slice x16, local copies, waits for them, and re-layouts, move_pages(): lax.dynamic_update_slice(page_pool, piece, (0, source * piece_rows, 0, 0))  21.5 us
    unnamed x12, local copies, waits for them, and re-layouts  11.1 us
    all_gather x1, waiting for transfers between devices, on_device(): ctx_all = lax.all_gather(ctx_rows, 'seq', axis=0, tiled=True)  10.8 us
  transfers between devices with their start and end apart: 19, of which 10 were waited for; matrix products, arithmetic and copies ran while one was open for 18% of the time, Pallas kernels for 7%

profile of v2, /device:TPU:1, one launch (start us, length us, event | category | flops | bytes accessed | tf_op | source)
XLA Modules:
  0.0 325.0 jit_solution(3217422729517096808)
XLA Ops:
  7.2 0.7 all-gather.4.cloned.1.call-update
  7.9 1.9 copy.157
  9.9 0.7 fusion.28
  11.0 0.7 fusion.27
  12.4 1.9 copy.111
  14.4 3.1 gather_fusion
  17.5 2.9 copy.112
  20.5 0.8 fusion.4
  21.3 1.7 slice_bitcast_fusion
  23.0 5.0 %collective-permute-start = (bf16[4,128,2,128]{3,1,2,0:T(8,128)(2,1)}, bf16[4,128,2,128]{3,1,2,0:T(8,128)(2,1)}, u32[]{:S(2)}, u32[]{:S(2)}) collective-permute-start(bf16[4,128,2,128]{3,1,2,0:T(8,128)(2,1)} %get-tuple-element.30), channel_id=1, source_target_pairs={{0,8},{8,16},{16,24},{24,32},{32,40},{40,48},{48,56},{56,64},{64,7... | collective-permute-start | bytes 786440 | tf_op jit(solution)/shard_map/ppermute | solution.py:155
  27.9 0.3 collective-permute-start.1
  28.2 1.2 collective-permute-start.2
  29.4 1.2 collective-permute-start.3
  30.6 3.6 %collective-permute-start.4 = (bf16[4,128,2,128]{3,1,2,0:T(8,128)(2,1)}, bf16[4,128,2,128]{3,1,2,0:T(8,128)(2,1)}, u32[]{:S(2)}, u32[]{:S(2)}) collective-permute-start(bf16[4,128,2,128]{3,1,2,0:T(8,128)(2,1)} %get-tuple-element.26), channel_id=1, source_target_pairs={{0,40},{8,48},{16,56},{24,64},{32,72},{40,80},{48,88},{56,96},{64,... | collective-permute-start | bytes 786440 | tf_op jit(solution)/shard_map/ppermute | solution.py:155
  34.9 2.3 broadcast_in_dim.72
  37.2 0.3 copy_dynamic-update-slice_fusion.15
  37.5 0.3 multiply_cosine_fusion.1
  37.8 1.7 copy-done.1
  39.6 2.1 copy.156
  41.7 2.9 copy.108
  44.6 12.3 %collective-permute-done = bf16[4,128,2,128]{3,1,2,0:T(8,128)(2,1)} collective-permute-done((bf16[4,128,2,128]{3,1,2,0:T(8,128)(2,1)}, bf16[4,128,2,128]{3,1,2,0:T(8,128)(2,1)}, u32[]{:S(2)}, u32[]{:S(2)}) %collective-permute-start) | collective-permute-done | bytes 262176 | tf_op jit(solution)/shard_map/ppermute | solution.py:155
  56.9 1.9 copy_dynamic-update-slice_fusion.14
  58.8 9.3 %collective-permute-done.1 = bf16[4,128,2,128]{3,1,2,0:T(8,128)(2,1)} collective-permute-done((bf16[4,128,2,128]{3,1,2,0:T(8,128)(2,1)}, bf16[4,128,2,128]{3,1,2,0:T(8,128)(2,1)}, u32[]{:S(2)}, u32[]{:S(2)}) %collective-permute-start.1) | collective-permute-done | bytes 262176 | tf_op jit(solution)/shard_map/ppermute | solution.py:155
  68.1 1.9 copy_dynamic-update-slice_fusion.13
  70.0 2.3 fusion.1
  72.4 3.5 %fusion.7 = f32[256,2,1,128]{3,0,2,1:T(8,128)S(1)} fusion(bf16[2,128,5120]{2,1,0:T(8,128)(2,1)} %bitcast.99, bf16[256,5120]{1,0:T(8,128)(2,1)} %all-gather.4.cloned.1.call-done, f32[5120]{0:T(1024)} %param.10, f32[256]{0:T(256)S(1)} %add_rsqrt_fusion), kind=kOutput, calls=%fused_computation.13 | convolution fusion | flops 676331520 | bytes 5526528 | tf_op jit(solution)/shard_map/dot_general | solution.py:200
  75.9 0.6 fusion.23
  76.5 0.8 pad_maximum_fusion
  77.4 2.8 collective-permute-start.7
  80.1 1.9 copy_dynamic-update-slice_fusion.12
  82.1 5.9 %collective-permute-start.8 = (bf16[4,128,2,128]{3,1,2,0:T(8,128)(2,1)}, bf16[4,128,2,128]{3,1,2,0:T(8,128)(2,1)S(1)}, u32[]{:S(2)}, u32[]{:S(2)}) collective-permute-start(bf16[4,128,2,128]{3,1,2,0:T(8,128)(2,1)} %get-tuple-element.22), channel_id=1, source_target_pairs={{0,72},{8,80},{16,88},{24,96},{32,104},{40,112},{48,120},{56,0},{6... | collective-permute-start | bytes 786440 | tf_op jit(solution)/shard_map/ppermute | solution.py:155
  88.0 1.9 copy_dynamic-update-slice_fusion.11
  89.9 2.5 collective-permute-start.9
  92.4 1.9 copy_dynamic-update-slice_fusion.10
  94.4 1.9 copy_dynamic-update-slice_fusion.9
  96.3 2.4 collective-permute-start.11
  98.7 1.9 copy_dynamic-update-slice_fusion.8
  100.6 3.3 %collective-permute-start.12 = (bf16[4,128,2,128]{3,1,2,0:T(8,128)(2,1)S(1)}, bf16[4,128,2,128]{3,1,2,0:T(8,128)(2,1)S(1)}, u32[]{:S(2)}, u32[]{:S(2)}) collective-permute-start(bf16[4,128,2,128]{3,1,2,0:T(8,128)(2,1)S(1)} %get-tuple-element.18), channel_id=1, source_target_pairs={{0,104},{8,112},{16,120},{24,0},{32,8},{40,16},{48,24},{56,32},{64... | collective-permute-start | bytes 786440 | tf_op jit(solution)/shard_map/ppermute | solution.py:155
  103.9 1.0 copy_dynamic-update-slice_fusion.7
  104.9 2.7 collective-permute-start.13
  107.6 1.0 copy_dynamic-update-slice_fusion.6
  108.6 1.0 collective-permute-done.9
  109.6 1.9 collective-permute-start.14
  111.5 1.0 copy_dynamic-update-slice_fusion.5
  112.5 4.0 %collective-permute-done.10 = bf16[4,128,2,128]{3,1,2,0:T(8,128)(2,1)S(1)} collective-permute-done((bf16[4,128,2,128]{3,1,2,0:T(8,128)(2,1)}, bf16[4,128,2,128]{3,1,2,0:T(8,128)(2,1)S(1)}, u32[]{:S(2)}, u32[]{:S(2)}) %collective-permute-start.10) | collective-permute-done | bytes 262176 | tf_op jit(solution)/shard_map/ppermute | solution.py:155
  116.4 1.0 copy_dynamic-update-slice_fusion.4
  117.4 7.6 %collective-permute-done.11 = bf16[4,128,2,128]{3,1,2,0:T(8,128)(2,1)S(1)} collective-permute-done((bf16[4,128,2,128]{3,1,2,0:T(8,128)(2,1)}, bf16[4,128,2,128]{3,1,2,0:T(8,128)(2,1)S(1)}, u32[]{:S(2)}, u32[]{:S(2)}) %collective-permute-start.11) | collective-permute-done | bytes 262176 | tf_op jit(solution)/shard_map/ppermute | solution.py:155
  125.0 1.0 copy_dynamic-update-slice_fusion.3
  126.0 5.6 %collective-permute-done.12 = bf16[4,128,2,128]{3,1,2,0:T(8,128)(2,1)S(1)} collective-permute-done((bf16[4,128,2,128]{3,1,2,0:T(8,128)(2,1)S(1)}, bf16[4,128,2,128]{3,1,2,0:T(8,128)(2,1)S(1)}, u32[]{:S(2)}, u32[]{:S(2)}) %collective-permute-start.12) | collective-permute-done | bytes 262176 | tf_op jit(solution)/shard_map/ppermute | solution.py:155
  131.5 1.0 copy_dynamic-update-slice_fusion.2
  132.5 6.8 %collective-permute-done.13 = bf16[4,128,2,128]{3,1,2,0:T(8,128)(2,1)S(1)} collective-permute-done((bf16[4,128,2,128]{3,1,2,0:T(8,128)(2,1)S(1)}, bf16[4,128,2,128]{3,1,2,0:T(8,128)(2,1)S(1)}, u32[]{:S(2)}, u32[]{:S(2)}) %collective-permute-start.13) | collective-permute-done | bytes 262176 | tf_op jit(solution)/shard_map/ppermute | solution.py:155
  139.3 1.0 copy_dynamic-update-slice_fusion.1
  140.3 1.0 copy_dynamic-update-slice_fusion
  141.3 5.9 %fusion.11 = f32[256,640]{0,1:T(8,128)S(1)} fusion(bf16[5120,640]{1,0:T(8,128)(2,1)} %param.11, bf16[256,5120]{1,0:T(8,128)(2,1)S(1)} %copy-done.2, f32[5120]{0:T(1024)S(1)} %copy-done.3, f32[256]{0:T(256)S(1)} %add_rsqrt_fusion), kind=kOutput, calls=%fused_computation.14 | convolution fusion | flops 1682964480 | bytes 9851904 | tf_op jit(solution)/shard_map/dot_general | solution.py:195
  147.5 10.8 %all-gather.8.cloned.1.call-done.kv_ref = bf16[16384,256]{1,0:T(8,128)(2,1)} async-done(((bf16[1024,256]{1,0:T(8,128)(2,1)}), bf16[16384,256]{1,0:T(8,128)(2,1)}) %all-gather.8.cloned.1.call-update) | async-done | bytes 8388624 | tf_op jit(solution)/shard_map/all_gather | solution.py:181
  158.5 23.1 %shard_map.104 = (f32[1280,1]{1,0:T(8,128)S(1)}, f32[1280,1]{1,0:T(8,128)S(1)}, f32[1280,128]{1,0:T(8,128)S(1)}) custom-call(s32[2]{0:T(128)S(1)} %pad_add_fusion.scalars, bf16[1280,128]{1,0:T(8,128)(2,1)S(1)} %bitcast.93, bf16[16384,256]{1,0:T(8,128)(2,1)} %all-gather.8.cloned.1.call-done.kv_ref, f32[1280,1]{1,0:T(8,128)S(1)} %broadcast_in_dim.84.m_in, ...), custom_call_target="tpu_custom_call" | custom-call | tf_op jit(solution)/shard_map/pallas_call | solution.py:100
  181.6 30.7 %all-gather.6.cloned.1.call-done.kv_ref = bf16[4096,256]{1,0:T(8,128)(2,1)} async-done(((bf16[256,256]{1,0:T(8,128)(2,1)}), bf16[4096,256]{1,0:T(8,128)(2,1)}) %all-gather.6.cloned.1.call-update) | async-done | bytes 2097168 | tf_op jit(solution)/shard_map/all_gather | solution.py:208
  212.3 9.5 %shard_map.105 = (f32[1280,1]{1,0:T(8,128)}, f32[1280,1]{1,0:T(8,128)S(1)}, f32[1280,128]{1,0:T(8,128)S(1)}) custom-call(s32[2]{0:T(128)S(1)} %pad_add_fusion.scalars, bf16[1280,128]{1,0:T(8,128)(2,1)S(1)} %bitcast.94, bf16[4096,256]{1,0:T(8,128)(2,1)} %all-gather.6.cloned.1.call-done.kv_ref, f32[1280,1]{1,0:T(8,128)S(1)} %get-tuple-element.10.m_in, ...), custom_call_target="tpu_custom_call" | custom-call | tf_op jit(solution)/shard_map/pallas_call | solution.py:100
  221.8 0.8 copy-done
  222.8 1.3 divide_convert_fusion
  224.4 5.1 %fusion = bf16[5120,256]{0,1:T(8,128)(2,1)S(1)} fusion(bf16[256,640]{0,1:T(8,128)(2,1)S(1)} %bitcast.102, bf16[640,5120]{1,0:T(8,128)(2,1)} %param.13), kind=kOutput, calls=%fused_computation.4 | convolution fusion | flops 1679032320 | bytes 9502720 | tf_op jit(solution)/shard_map/dot_general | solution.py:225
  229.5 2.6 copy.134
  232.1 84.4 %reduce-scatter.4.cloned.1.call-done = bf16[640,256]{1,0:T(8,128)(2,1)} async-done(((bf16[5120,256]{1,0:T(8,128)(2,1)}), bf16[640,256]{1,0:T(8,128)(2,1)}) %reduce-scatter.4.cloned.1.call-update) | async-done | bytes 327696
  316.6 1.9 copy.135
  (53 shorter events, 2.4 us)
Async XLA Ops:
  7.2 62.9 %all-gather.4.cloned.1.call-start = ((), (), s32[]{:S(2)}) async-start(), calls=%async_computation.1 | async-start | bytes 2949120 | tf_op jit(solution)/shard_map/all_gather | solution.py:184
  7.9 150.4 %all-gather.8.cloned.1.call-start = ((), (), s32[]{:S(2)}) async-start(), calls=%async_computation.3 | async-start | bytes 8912896 | tf_op jit(solution)/shard_map/all_gather | solution.py:181
  9.9 202.4 %all-gather.6.cloned.1.call-start = ((), (), s32[]{:S(2)}) async-start(), calls=%async_computation.2 | async-start | bytes 2228224 | tf_op jit(solution)/shard_map/all_gather | solution.py:208
  23.0 33.9 %collective-permute-start = (bf16[4,128,2,128]{3,1,2,0:T(8,128)(2,1)}, bf16[4,128,2,128]{3,1,2,0:T(8,128)(2,1)}, u32[]{:S(2)}, u32[]{:S(2)}) collective-permute-start(bf16[4,128,2,128]{3,1,2,0:T(8,128)(2,1)} %get-tuple-element.30), channel_id=1, source_target_pairs={{0,8},{8,16},{16,24},{24,32},{32,40},{40,48},{48,56},{56,64},{64,7... | collective-permute-start | bytes 786440 | tf_op jit(solution)/shard_map/ppermute | solution.py:155
  27.9 40.2 %collective-permute-start.1 = (bf16[4,128,2,128]{3,1,2,0:T(8,128)(2,1)}, bf16[4,128,2,128]{3,1,2,0:T(8,128)(2,1)}, u32[]{:S(2)}, u32[]{:S(2)}) collective-permute-start(bf16[4,128,2,128]{3,1,2,0:T(8,128)(2,1)} %get-tuple-element.29), channel_id=1, source_target_pairs={{0,16},{8,24},{16,32},{24,40},{32,48},{40,56},{48,64},{56,72},{64,... | collective-permute-start | bytes 786440 | tf_op jit(solution)/shard_map/ppermute | solution.py:155
  28.2 49.1 %collective-permute-start.2 = (bf16[4,128,2,128]{3,1,2,0:T(8,128)(2,1)}, bf16[4,128,2,128]{3,1,2,0:T(8,128)(2,1)}, u32[]{:S(2)}, u32[]{:S(2)}) collective-permute-start(bf16[4,128,2,128]{3,1,2,0:T(8,128)(2,1)} %get-tuple-element.28), channel_id=1, source_target_pairs={{0,24},{8,32},{16,40},{24,48},{32,56},{40,64},{48,72},{56,80},{64,... | collective-permute-start | bytes 786440 | tf_op jit(solution)/shard_map/ppermute | solution.py:155
  29.4 52.6 %collective-permute-start.3 = (bf16[4,128,2,128]{3,1,2,0:T(8,128)(2,1)}, bf16[4,128,2,128]{3,1,2,0:T(8,128)(2,1)}, u32[]{:S(2)}, u32[]{:S(2)}) collective-permute-start(bf16[4,128,2,128]{3,1,2,0:T(8,128)(2,1)} %get-tuple-element.27), channel_id=1, source_target_pairs={{0,32},{8,40},{16,48},{24,56},{32,64},{40,72},{48,80},{56,88},{64,... | collective-permute-start | bytes 786440 | tf_op jit(solution)/shard_map/ppermute | solution.py:155
  30.6 59.3 %collective-permute-start.4 = (bf16[4,128,2,128]{3,1,2,0:T(8,128)(2,1)}, bf16[4,128,2,128]{3,1,2,0:T(8,128)(2,1)}, u32[]{:S(2)}, u32[]{:S(2)}) collective-permute-start(bf16[4,128,2,128]{3,1,2,0:T(8,128)(2,1)} %get-tuple-element.26), channel_id=1, source_target_pairs={{0,40},{8,48},{16,56},{24,64},{32,72},{40,80},{48,88},{56,96},{64,... | collective-permute-start | bytes 786440 | tf_op jit(solution)/shard_map/ppermute | solution.py:155
  37.5 2.0 copy-start.1
  56.9 37.5 %collective-permute-start.5 = (bf16[4,128,2,128]{3,1,2,0:T(8,128)(2,1)}, bf16[4,128,2,128]{3,1,2,0:T(8,128)(2,1)}, u32[]{:S(2)}, u32[]{:S(2)}) collective-permute-start(bf16[4,128,2,128]{3,1,2,0:T(8,128)(2,1)} %get-tuple-element.25), channel_id=1, source_target_pairs={{0,48},{8,56},{16,64},{24,72},{32,80},{40,88},{48,96},{56,104},{64... | collective-permute-start | bytes 786440 | tf_op jit(solution)/shard_map/ppermute | solution.py:155
  68.1 28.2 %collective-permute-start.6 = (bf16[4,128,2,128]{3,1,2,0:T(8,128)(2,1)}, bf16[4,128,2,128]{3,1,2,0:T(8,128)(2,1)}, u32[]{:S(2)}, u32[]{:S(2)}) collective-permute-start(bf16[4,128,2,128]{3,1,2,0:T(8,128)(2,1)} %get-tuple-element.24), channel_id=1, source_target_pairs={{0,56},{8,64},{16,72},{24,80},{32,88},{40,96},{48,104},{56,112},{6... | collective-permute-start | bytes 786440 | tf_op jit(solution)/shard_map/ppermute | solution.py:155
  75.9 65.4 %copy-start.2 = (bf16[256,5120]{1,0:T(8,128)(2,1)S(1)}, bf16[256,5120]{1,0:T(8,128)(2,1)}, u32[]{:S(2)}) copy-start(bf16[256,5120]{1,0:T(8,128)(2,1)} %all-gather.4.cloned.1.call-done) | copy-start | bytes 7864324
  77.3 239.3 %reduce-scatter.4.cloned.1.call-start = ((), (), s32[]{:S(2)}) async-start(), calls=%async_computation.4 | async-start | bytes 2949120
  77.3 63.9 %copy-start.3 = (f32[5120]{0:T(1024)S(1)}, f32[5120]{0:T(1024)}, u32[]{:S(2)}) copy-start(f32[5120]{0:T(1024)} %param.10) | copy-start | bytes 61444
  77.4 23.3 %collective-permute-start.7 = (bf16[4,128,2,128]{3,1,2,0:T(8,128)(2,1)}, bf16[4,128,2,128]{3,1,2,0:T(8,128)(2,1)S(1)}, u32[]{:S(2)}, u32[]{:S(2)}) collective-permute-start(bf16[4,128,2,128]{3,1,2,0:T(8,128)(2,1)} %get-tuple-element.23), channel_id=1, source_target_pairs={{0,64},{8,72},{16,80},{24,88},{32,96},{40,104},{48,112},{56,120},{... | collective-permute-start | bytes 786440 | tf_op jit(solution)/shard_map/ppermute | solution.py:155
  82.1 22.8 %collective-permute-start.8 = (bf16[4,128,2,128]{3,1,2,0:T(8,128)(2,1)}, bf16[4,128,2,128]{3,1,2,0:T(8,128)(2,1)S(1)}, u32[]{:S(2)}, u32[]{:S(2)}) collective-permute-start(bf16[4,128,2,128]{3,1,2,0:T(8,128)(2,1)} %get-tuple-element.22), channel_id=1, source_target_pairs={{0,72},{8,80},{16,88},{24,96},{32,104},{40,112},{48,120},{56,0},{6... | collective-permute-start | bytes 786440 | tf_op jit(solution)/shard_map/ppermute | solution.py:155
  89.9 19.6 %collective-permute-start.9 = (bf16[4,128,2,128]{3,1,2,0:T(8,128)(2,1)}, bf16[4,128,2,128]{3,1,2,0:T(8,128)(2,1)S(1)}, u32[]{:S(2)}, u32[]{:S(2)}) collective-permute-start(bf16[4,128,2,128]{3,1,2,0:T(8,128)(2,1)} %get-tuple-element.21), channel_id=1, source_target_pairs={{0,80},{8,88},{16,96},{24,104},{32,112},{40,120},{48,0},{56,8},{64... | collective-permute-start | bytes 786440 | tf_op jit(solution)/shard_map/ppermute | solution.py:155
  94.3 22.1 %collective-permute-start.10 = (bf16[4,128,2,128]{3,1,2,0:T(8,128)(2,1)}, bf16[4,128,2,128]{3,1,2,0:T(8,128)(2,1)S(1)}, u32[]{:S(2)}, u32[]{:S(2)}) collective-permute-start(bf16[4,128,2,128]{3,1,2,0:T(8,128)(2,1)} %get-tuple-element.20), channel_id=1, source_target_pairs={{0,88},{8,96},{16,104},{24,112},{32,120},{40,0},{48,8},{56,16},{64... | collective-permute-start | bytes 786440 | tf_op jit(solution)/shard_map/ppermute | solution.py:155
  96.3 28.7 %collective-permute-start.11 = (bf16[4,128,2,128]{3,1,2,0:T(8,128)(2,1)}, bf16[4,128,2,128]{3,1,2,0:T(8,128)(2,1)S(1)}, u32[]{:S(2)}, u32[]{:S(2)}) collective-permute-start(bf16[4,128,2,128]{3,1,2,0:T(8,128)(2,1)} %get-tuple-element.19), channel_id=1, source_target_pairs={{0,96},{8,104},{16,112},{24,120},{32,0},{40,8},{48,16},{56,24},{64... | collective-permute-start | bytes 786440 | tf_op jit(solution)/shard_map/ppermute | solution.py:155
  100.6 30.9 %collective-permute-start.12 = (bf16[4,128,2,128]{3,1,2,0:T(8,128)(2,1)S(1)}, bf16[4,128,2,128]{3,1,2,0:T(8,128)(2,1)S(1)}, u32[]{:S(2)}, u32[]{:S(2)}) collective-permute-start(bf16[4,128,2,128]{3,1,2,0:T(8,128)(2,1)S(1)} %get-tuple-element.18), channel_id=1, source_target_pairs={{0,104},{8,112},{16,120},{24,0},{32,8},{40,16},{48,24},{56,32},{64... | collective-permute-start | bytes 786440 | tf_op jit(solution)/shard_map/ppermute | solution.py:155
  104.9 34.5 %collective-permute-start.13 = (bf16[4,128,2,128]{3,1,2,0:T(8,128)(2,1)S(1)}, bf16[4,128,2,128]{3,1,2,0:T(8,128)(2,1)S(1)}, u32[]{:S(2)}, u32[]{:S(2)}) collective-permute-start(bf16[4,128,2,128]{3,1,2,0:T(8,128)(2,1)S(1)} %get-tuple-element.17), channel_id=1, source_target_pairs={{0,112},{8,120},{16,0},{24,8},{32,16},{40,24},{48,32},{56,40},{64,... | collective-permute-start | bytes 786440 | tf_op jit(solution)/shard_map/ppermute | solution.py:155
  109.6 30.7 %collective-permute-start.14 = (bf16[4,128,2,128]{3,1,2,0:T(8,128)(2,1)S(1)}, bf16[4,128,2,128]{3,1,2,0:T(8,128)(2,1)S(1)}, u32[]{:S(2)}, u32[]{:S(2)}) collective-permute-start(bf16[4,128,2,128]{3,1,2,0:T(8,128)(2,1)S(1)} %get-tuple-element.16), channel_id=1, source_target_pairs={{0,120},{8,0},{16,8},{24,16},{32,24},{40,32},{48,40},{56,48},{64,5... | collective-permute-start | bytes 786440 | tf_op jit(solution)/shard_map/ppermute | solution.py:155
  221.8 0.8 copy-start
Sparse Core Ops, SparseCore 0:
  9.6 44.2 all-gather.3
  56.3 102.0 all-gather.7
  160.7 51.4 all-gather.5
  232.2 84.2 reduce-scatter.3

commit v3 on v2

--- a/solution.py
+++ b/solution.py
@@ -55,8 +55,10 @@
 
     if causal:
         live = step <= seq_place
+        key_first = (seq_place - step) * block_rows
     else:
-        live = step * block_rows < span_first
+        key_first = step * block_rows
+        live = key_first < span_first
 
     @pl.when(live)
     def _():
@@ -66,7 +68,7 @@
         scores = lax.dot_general(
             q, k, (((1,), (1,)), ((), ())), preferred_element_type=jnp.float32
         ) * HD ** (-0.5)
-        col = lax.broadcasted_iota(jnp.int32, scores.shape, 1) + step * block_rows
+        col = lax.broadcasted_iota(jnp.int32, scores.shape, 1) + key_first
         if causal:
             row = (lax.broadcasted_iota(jnp.int32, scores.shape, 0) & (tok_rows - 1)) + seq_place * tok_rows
             visible = col <= row
@@ -205,7 +207,12 @@
     )
     new_values = projected[:, 1].astype(jnp.bfloat16).reshape(tok_rows, kv_width)
     new_rows = jnp.concatenate([new_keys, new_values], 1)
-    new_all = lax.all_gather(new_rows, "seq", axis=0, tiled=True)
+    arrived = [new_rows]
+    for shift in range(1, seq_count):
+        arrived.append(
+            lax.ppermute(new_rows, "seq", [(s, s + shift) for s in range(seq_count - shift)])
+        )
+    new_all = jnp.concatenate(arrived, 0)
     query_rows = head_group * tok_rows
     scalars = jnp.stack([span_first, seq_place]).astype(jnp.int32)
     empty_state = (
@@ -221,15 +228,20 @@
         .reshape(head_group, tok_rows, HD)
     )
     mixed_heads = jnp.transpose(mixed_heads, (1, 0, 2)).reshape(tok_rows, kv_width * head_group)
-    reduced = lax.psum_scatter(
-        lax.dot_general(
-            out_weight, mixed_heads, (((0,), (1,)), ((), ())), preferred_element_type=jnp.float32
-        ).astype(jnp.bfloat16),
-        "tp",
-        scatter_dimension=0,
-        tiled=True,
-    ).astype(jnp.float32)
-    attended = reduced.T.astype(jnp.bfloat16)
+    tp_count = lax.axis_size("tp")
+    tp_place = lax.axis_index("tp")
+    out_cols = out_weight.shape[1] // tp_count
+    partial = jnp.dot(mixed_heads, out_weight, preferred_element_type=jnp.float32)
+    reduced = lax.dynamic_slice_in_dim(partial, tp_place * out_cols, out_cols, 1)
+    partial = partial.astype(jnp.bfloat16)
+    for shift in range(1, tp_count):
+        chunk = lax.dynamic_slice_in_dim(
+            partial, ((tp_place + shift) % tp_count) * out_cols, out_cols, 1
+        )
+        reduced = reduced + lax.ppermute(
+            chunk, "tp", [(i, (i + shift) % tp_count) for i in range(tp_count)]
+        ).astype(jnp.float32)
+    attended = reduced.astype(jnp.bfloat16)
     return (attended, page_pool)
 
 

time: 330 us -> 325 us (0.985)
  the two profiles are of different devices: /device:TPU:1 before, /device:TPU:71 now
where the time goes in v3:
time: 325 us; the launch traced here: 327 us
  Pallas kernels  85.4 us (26%)
  starting transfers between devices  80 us (25%)
  waiting for transfers between devices  78.6 us (24%)
  local copies, waits for them, and re-layouts  42.6 us (13%)
  matrix products  16.2 us (5%)
  between operations  15.3 us (5%)
  other arithmetic  9.11 us (3%)
    pallas_call x2, Pallas kernels, flash_pass(): pl.pallas_call(kernel, out_shape=(jax.ShapeDtypeStruct((rows, 1), jnp.flo...  85.4 us
    ppermute x15, starting transfers between devices, move_pages(): lax.ppermute(piece, 'seq', [(s, (s + shift) % seq_count) for s in range(s...  48.9 us
    ppermute x15, waiting for transfers between devices, move_pages(): lax.ppermute(piece, 'seq', [(s, (s + shift) % seq_count) for s in range(s...  31.4 us
    ppermute x15, waiting for transfers between devices, on_device(): lax.ppermute(new_rows, 'seq', [(s, s + shift) for s in range(seq_count -...  23.7 us
    ppermute x7, waiting for transfers between devices, on_device(): lax.ppermute(chunk, 'tp', [(i, (i + shift) % tp_count) for i in range(tp_...  22.8 us
    dynamic_update_slice x16, local copies, waits for them, and re-layouts, move_pages(): lax.dynamic_update_slice(page_pool, piece, (0, source * piece_rows, 0, 0))  19.6 us
    ppermute x15, starting transfers between devices, on_device(): lax.ppermute(new_rows, 'seq', [(s, s + shift) for s in range(seq_count -...  19.5 us
    ppermute x7, starting transfers between devices, on_device(): lax.ppermute(chunk, 'tp', [(i, (i + shift) % tp_count) for i in range(tp_...  11.5 us
  transfers between devices with their start and end apart: 39, of which 20 were waited for; matrix products, arithmetic and copies ran while one was open for 17% of the time, Pallas kernels for 0%

profile of v3, /device:TPU:71, one launch (start us, length us, event | category | flops | bytes accessed | tf_op | source)
XLA Modules:
  0.0 327.2 jit_solution(9584818658139767679)
XLA Ops:
  7.9 1.9 copy.131
  12.4 1.9 copy.87
  14.3 3.1 gather_fusion
  17.5 2.9 copy.88
  21.2 1.7 slice_bitcast_fusion
  22.9 3.4 %collective-permute-start.16 = (bf16[4,128,2,128]{3,1,2,0:T(8,128)(2,1)}, bf16[4,128,2,128]{3,1,2,0:T(8,128)(2,1)}, u32[]{:S(2)}, u32[]{:S(2)}) collective-permute-start(bf16[4,128,2,128]{3,1,2,0:T(8,128)(2,1)} %get-tuple-element.31), channel_id=1, source_target_pairs={{0,16},{8,24},{16,32},{24,40},{32,48},{40,56},{48,64},{56,72},{64,... | collective-permute-start | bytes 786440 | tf_op jit(solution)/shard_map/ppermute | solution.py:157
  26.3 1.2 collective-permute-start.18
  27.6 5.1 %collective-permute-start.19 = (bf16[4,128,2,128]{3,1,2,0:T(8,128)(2,1)}, bf16[4,128,2,128]{3,1,2,0:T(8,128)(2,1)}, u32[]{:S(2)}, u32[]{:S(2)}) collective-permute-start(bf16[4,128,2,128]{3,1,2,0:T(8,128)(2,1)} %get-tuple-element.28), channel_id=1, source_target_pairs={{0,40},{8,48},{16,56},{24,64},{32,72},{40,80},{48,88},{56,96},{64,... | collective-permute-start | bytes 786440 | tf_op jit(solution)/shard_map/ppermute | solution.py:157
  33.3 2.3 broadcast_in_dim.72
  36.2 1.7 copy-done
  38.0 2.1 copy.130
  40.1 2.9 copy.84
  43.0 13.3 %collective-permute-start.20 = (bf16[4,128,2,128]{3,1,2,0:T(8,128)(2,1)}, bf16[4,128,2,128]{3,1,2,0:T(8,128)(2,1)S(1)}, u32[]{:S(2)}, u32[]{:S(2)}) collective-permute-start(bf16[4,128,2,128]{3,1,2,0:T(8,128)(2,1)} %get-tuple-element.27), channel_id=1, source_target_pairs={{0,48},{8,56},{16,64},{24,72},{32,80},{40,88},{48,96},{56,104},{64... | collective-permute-start | bytes 786440 | tf_op jit(solution)/shard_map/ppermute | solution.py:157
  56.3 1.9 copy_dynamic-update-slice_fusion.14
  58.2 8.9 %collective-permute-done.16 = bf16[4,128,2,128]{3,1,2,0:T(8,128)(2,1)} collective-permute-done((bf16[4,128,2,128]{3,1,2,0:T(8,128)(2,1)}, bf16[4,128,2,128]{3,1,2,0:T(8,128)(2,1)}, u32[]{:S(2)}, u32[]{:S(2)}) %collective-permute-start.16) | collective-permute-done | bytes 262176 | tf_op jit(solution)/shard_map/ppermute | solution.py:157
  67.0 1.9 copy_dynamic-update-slice_fusion.13
  69.0 1.2 collective-permute-start.22
  70.1 1.9 copy_dynamic-update-slice_fusion.12
  72.1 3.8 %collective-permute-start.23 = (bf16[4,128,2,128]{3,1,2,0:T(8,128)(2,1)}, bf16[4,128,2,128]{3,1,2,0:T(8,128)(2,1)S(1)}, u32[]{:S(2)}, u32[]{:S(2)}) collective-permute-start(bf16[4,128,2,128]{3,1,2,0:T(8,128)(2,1)} %get-tuple-element.24), channel_id=1, source_target_pairs={{0,72},{8,80},{16,88},{24,96},{32,104},{40,112},{48,120},{56,0},{6... | collective-permute-start | bytes 786440 | tf_op jit(solution)/shard_map/ppermute | solution.py:157
  75.9 1.9 copy_dynamic-update-slice_fusion.11
  78.9 1.9 copy_dynamic-update-slice_fusion.10
  81.9 1.8 collective-permute-start.26
  84.7 4.9 %collective-permute-start.27 = (bf16[4,128,2,128]{3,1,2,0:T(8,128)(2,1)S(1)}, bf16[4,128,2,128]{3,1,2,0:T(8,128)(2,1)S(1)}, u32[]{:S(2)}, u32[]{:S(2)}) collective-permute-start(bf16[4,128,2,128]{3,1,2,0:T(8,128)(2,1)S(1)} %get-tuple-element.20), channel_id=1, source_target_pairs={{0,104},{8,112},{16,120},{24,0},{32,8},{40,16},{48,24},{56,32},{64... | collective-permute-start | bytes 786440 | tf_op jit(solution)/shard_map/ppermute | solution.py:157
  90.6 1.5 collective-permute-done.23
  93.4 5.1 %collective-permute-done.24 = bf16[4,128,2,128]{3,1,2,0:T(8,128)(2,1)S(1)} collective-permute-done((bf16[4,128,2,128]{3,1,2,0:T(8,128)(2,1)}, bf16[4,128,2,128]{3,1,2,0:T(8,128)(2,1)S(1)}, u32[]{:S(2)}, u32[]{:S(2)}) %collective-permute-start.24) | collective-permute-done | bytes 262176 | tf_op jit(solution)/shard_map/ppermute | solution.py:157
  98.5 12.5 %collective-permute-start.29 = (bf16[4,128,2,128]{3,1,2,0:T(8,128)(2,1)S(1)}, bf16[4,128,2,128]{3,1,2,0:T(8,128)(2,1)S(1)}, u32[]{:S(2)}, u32[]{:S(2)}) collective-permute-start(bf16[4,128,2,128]{3,1,2,0:T(8,128)(2,1)S(1)} %get-tuple-element.18), channel_id=1, source_target_pairs={{0,120},{8,0},{16,8},{24,16},{32,24},{40,32},{48,40},{56,48},{64,5... | collective-permute-start | bytes 786440 | tf_op jit(solution)/shard_map/ppermute | solution.py:157
  113.0 1.1 collective-permute-done.26
  116.0 14.7 %collective-permute-done.28 = bf16[4,128,2,128]{3,1,2,0:T(8,128)(2,1)S(1)} collective-permute-done((bf16[4,128,2,128]{3,1,2,0:T(8,128)(2,1)S(1)}, bf16[4,128,2,128]{3,1,2,0:T(8,128)(2,1)S(1)}, u32[]{:S(2)}, u32[]{:S(2)}) %collective-permute-start.28) | collective-permute-done | bytes 262176 | tf_op jit(solution)/shard_map/ppermute | solution.py:157
  132.8 2.3 fusion
  135.2 3.0 fusion.6
  138.9 1.3 collective-permute-start
  140.2 1.3 collective-permute-start.1
  141.5 1.3 collective-permute-start.2
  142.8 1.3 collective-permute-start.3
  144.1 1.3 collective-permute-start.4
  145.5 5.8 %fusion.10 = f32[256,640]{0,1:T(8,128)S(1)} fusion(bf16[5120,640]{1,0:T(8,128)(2,1)} %param.11, bf16[256,5120]{1,0:T(8,128)(2,1)S(1)} %copy-done.1, f32[5120]{0:T(1024)S(1)} %copy-done.4, f32[256]{0:T(256)S(1)} %add_rsqrt_fusion), kind=kOutput, calls=%fused_computation.12 | convolution fusion | flops 1682964480 | bytes 9851904 | tf_op jit(solution)/shard_map/dot_general | solution.py:197
  151.6 1.3 collective-permute-start.5
  153.8 1.3 collective-permute-start.6
  155.2 1.3 collective-permute-start.7
  156.5 1.3 collective-permute-start.8
  157.8 4.2 %collective-permute-done.4 = bf16[256,256]{1,0:T(8,128)(2,1)S(1)} collective-permute-done((bf16[256,256]{1,0:T(8,128)(2,1)S(1)}, bf16[256,256]{1,0:T(8,128)(2,1)S(1)}, u32[]{:S(2)}, u32[]{:S(2)}) %collective-permute-start.4) | collective-permute-done | bytes 131104 | tf_op jit(solution)/shard_map/ppermute | solution.py:213
  162.1 1.3 collective-permute-start.9
  163.4 1.6 collective-permute-done.5
  164.9 1.3 collective-permute-start.10
  166.2 1.3 collective-permute-done.6
  167.5 1.3 collective-permute-start.11
  168.8 3.3 collective-permute-done.7
  172.1 1.3 collective-permute-start.12
  173.4 1.3 collective-permute-start.13
  174.7 1.4 collective-permute-done.9
  176.2 1.5 collective-permute-start.14
  178.5 6.0 %collective-permute-done.11 = bf16[256,256]{1,0:T(8,128)(2,1)S(1)} collective-permute-done((bf16[256,256]{1,0:T(8,128)(2,1)S(1)}, bf16[256,256]{1,0:T(8,128)(2,1)S(1)}, u32[]{:S(2)}, u32[]{:S(2)}) %collective-permute-start.11) | collective-permute-done | bytes 131104 | tf_op jit(solution)/shard_map/ppermute | solution.py:213
  184.7 4.9 %collective-permute-done.13 = bf16[256,256]{1,0:T(8,128)(2,1)S(1)} collective-permute-done((bf16[256,256]{1,0:T(8,128)(2,1)S(1)}, bf16[256,256]{1,0:T(8,128)(2,1)S(1)}, u32[]{:S(2)}, u32[]{:S(2)}) %collective-permute-start.13) | collective-permute-done | bytes 131104 | tf_op jit(solution)/shard_map/ppermute | solution.py:213
  189.8 29.7 %shard_map.104 = (f32[1280,1]{1,0:T(8,128)S(1)}, f32[1280,1]{1,0:T(8,128)S(1)}, f32[1280,128]{1,0:T(8,128)S(1)}) custom-call(s32[2]{0:T(128)S(1)} %pad_add_fusion.scalars, bf16[1280,128]{1,0:T(8,128)(2,1)S(1)} %bitcast.89, bf16[16384,256]{1,0:T(8,128)(2,1)} %all-gather.5.cloned.1.call-done.kv_ref, f32[1280,1]{1,0:T(8,128)S(1)} %broadcast_in_dim.84.m_in, ...), custom_call_target="tpu_custom_call" | custom-call | tf_op jit(solution)/shard_map/pallas_call | solution.py:102
  219.6 55.7 %shard_map.105 = (f32[1280,1]{1,0:T(8,128)}, f32[1280,1]{1,0:T(8,128)S(1)}, f32[1280,128]{1,0:T(8,128)S(1)}) custom-call(s32[2]{0:T(128)S(1)} %pad_add_fusion.scalars, bf16[1280,128]{1,0:T(8,128)(2,1)S(1)} %bitcast.90, bf16[4096,256]{1,0:T(8,128)(2,1)} %copy-done.3, f32[1280,1]{1,0:T(8,128)S(1)} %get-tuple-element.10.m_in, ...), custom_call_target="tpu_custom_call" | custom-call | tf_op jit(solution)/shard_map/pallas_call | solution.py:102
  276.0 7.4 %fusion.31 = (bf16[256,5120]{1,0:T(8,128)(2,1)S(1)}, f32[256,5120]{1,0:T(8,128)}) fusion(bf16[256,640]{0,1:T(8,128)(2,1)S(1)} %bitcast.98, bf16[640,5120]{1,0:T(8,128)(2,1)} %param.13), kind=kOutput, calls=%fused_computation.118 | convolution fusion | flops 1679032320 | bytes 14745600 | tf_op jit(solution)/shard_map/dot_general | solution.py:234
  283.7 3.6 %collective-permute-start.36 = (bf16[256,640]{1,0:T(8,128)(2,1)S(1)}, bf16[256,640]{1,0:T(8,128)(2,1)S(1)}, u32[]{:S(2)}, u32[]{:S(2)}) collective-permute-start(bf16[256,640]{1,0:T(8,128)(2,1)S(1)} %get-tuple-element.35), channel_id=1, source_target_pairs={{0,7},{1,0},{2,1},{3,2},{4,3},{5,4},{6,5},{7,6},{8,15},{9,8},{10,9... | collective-permute-start | bytes 983048 | tf_op jit(solution)/shard_map/ppermute | solution.py:241
  287.3 1.7 collective-permute-start.34
  289.1 2.2 collective-permute-start.32
  291.3 14.3 %collective-permute-done.36 = bf16[256,640]{1,0:T(8,128)(2,1)S(1)} collective-permute-done((bf16[256,640]{1,0:T(8,128)(2,1)S(1)}, bf16[256,640]{1,0:T(8,128)(2,1)S(1)}, u32[]{:S(2)}, u32[]{:S(2)}) %collective-permute-start.36) | collective-permute-done | bytes 327712 | tf_op jit(solution)/shard_map/ppermute | solution.py:241
  305.6 3.9 %collective-permute-start.30 = (bf16[256,640]{1,0:T(8,128)(2,1)S(1)}, bf16[256,640]{1,0:T(8,128)(2,1)}, u32[]{:S(2)}, u32[]{:S(2)}) collective-permute-start(bf16[256,640]{1,0:T(8,128)(2,1)S(1)} %get-tuple-element.34), channel_id=1, source_target_pairs={{0,1},{1,2},{2,3},{3,4},{4,5},{5,6},{6,7},{7,0},{8,9},{9,10},{10,1... | collective-permute-start | bytes 983048 | tf_op jit(solution)/shard_map/ppermute | solution.py:241
  309.5 4.4 %collective-permute-done.32 = bf16[256,640]{1,0:T(8,128)(2,1)S(1)} collective-permute-done((bf16[256,640]{1,0:T(8,128)(2,1)S(1)}, bf16[256,640]{1,0:T(8,128)(2,1)S(1)}, u32[]{:S(2)}, u32[]{:S(2)}) %collective-permute-start.32) | collective-permute-done | bytes 327712 | tf_op jit(solution)/shard_map/ppermute | solution.py:241
  314.6 3.4 %collective-permute-done.30 = bf16[256,640]{1,0:T(8,128)(2,1)} collective-permute-done((bf16[256,640]{1,0:T(8,128)(2,1)S(1)}, bf16[256,640]{1,0:T(8,128)(2,1)}, u32[]{:S(2)}, u32[]{:S(2)}) %collective-permute-start.30) | collective-permute-done | bytes 327712 | tf_op jit(solution)/shard_map/ppermute | solution.py:241
  318.0 2.4 add_convert_fusion
  (108 shorter events, 21.3 us)
Async XLA Ops:
  7.2 125.7 %all-gather.3.cloned.1.call-start = ((), (), s32[]{:S(2)}) async-start(), calls=%async_computation | async-start | bytes 2949120 | tf_op jit(solution)/shard_map/all_gather | solution.py:186
  7.9 181.8 %all-gather.5.cloned.1.call-start = ((), (), s32[]{:S(2)}) async-start(), calls=%async_computation.1 | async-start | bytes 8912896 | tf_op jit(solution)/shard_map/all_gather | solution.py:183
  22.9 20.1 %collective-permute-start.15 = (bf16[4,128,2,128]{3,1,2,0:T(8,128)(2,1)}, bf16[4,128,2,128]{3,1,2,0:T(8,128)(2,1)}, u32[]{:S(2)}, u32[]{:S(2)}) collective-permute-start(bf16[4,128,2,128]{3,1,2,0:T(8,128)(2,1)} %get-tuple-element.32), channel_id=1, source_target_pairs={{0,8},{8,16},{16,24},{24,32},{32,40},{40,48},{48,56},{56,64},{64,7... | collective-permute-start | bytes 786440 | tf_op jit(solution)/shard_map/ppermute | solution.py:157
  22.9 44.1 %collective-permute-start.16 = (bf16[4,128,2,128]{3,1,2,0:T(8,128)(2,1)}, bf16[4,128,2,128]{3,1,2,0:T(8,128)(2,1)}, u32[]{:S(2)}, u32[]{:S(2)}) collective-permute-start(bf16[4,128,2,128]{3,1,2,0:T(8,128)(2,1)} %get-tuple-element.31), channel_id=1, source_target_pairs={{0,16},{8,24},{16,32},{24,40},{32,48},{40,56},{48,64},{56,72},{64,... | collective-permute-start | bytes 786440 | tf_op jit(solution)/shard_map/ppermute | solution.py:157
  26.3 42.6 %collective-permute-start.17 = (bf16[4,128,2,128]{3,1,2,0:T(8,128)(2,1)}, bf16[4,128,2,128]{3,1,2,0:T(8,128)(2,1)}, u32[]{:S(2)}, u32[]{:S(2)}) collective-permute-start(bf16[4,128,2,128]{3,1,2,0:T(8,128)(2,1)} %get-tuple-element.30), channel_id=1, source_target_pairs={{0,24},{8,32},{16,40},{24,48},{32,56},{40,64},{48,72},{56,80},{64,... | collective-permute-start | bytes 786440 | tf_op jit(solution)/shard_map/ppermute | solution.py:157
  26.3 45.7 %collective-permute-start.18 = (bf16[4,128,2,128]{3,1,2,0:T(8,128)(2,1)}, bf16[4,128,2,128]{3,1,2,0:T(8,128)(2,1)}, u32[]{:S(2)}, u32[]{:S(2)}) collective-permute-start(bf16[4,128,2,128]{3,1,2,0:T(8,128)(2,1)} %get-tuple-element.29), channel_id=1, source_target_pairs={{0,32},{8,40},{16,48},{24,56},{32,64},{40,72},{48,80},{56,88},{64,... | collective-permute-start | bytes 786440 | tf_op jit(solution)/shard_map/ppermute | solution.py:157
  27.6 50.3 %collective-permute-start.19 = (bf16[4,128,2,128]{3,1,2,0:T(8,128)(2,1)}, bf16[4,128,2,128]{3,1,2,0:T(8,128)(2,1)}, u32[]{:S(2)}, u32[]{:S(2)}) collective-permute-start(bf16[4,128,2,128]{3,1,2,0:T(8,128)(2,1)} %get-tuple-element.28), channel_id=1, source_target_pairs={{0,40},{8,48},{16,56},{24,64},{32,72},{40,80},{48,88},{56,96},{64,... | collective-permute-start | bytes 786440 | tf_op jit(solution)/shard_map/ppermute | solution.py:157
  35.9 2.0 copy-start
  43.0 37.8 %collective-permute-start.20 = (bf16[4,128,2,128]{3,1,2,0:T(8,128)(2,1)}, bf16[4,128,2,128]{3,1,2,0:T(8,128)(2,1)S(1)}, u32[]{:S(2)}, u32[]{:S(2)}) collective-permute-start(bf16[4,128,2,128]{3,1,2,0:T(8,128)(2,1)} %get-tuple-element.27), channel_id=1, source_target_pairs={{0,48},{8,56},{16,64},{24,72},{32,80},{40,88},{48,96},{56,104},{64... | collective-permute-start | bytes 786440 | tf_op jit(solution)/shard_map/ppermute | solution.py:157
  67.0 14.9 %collective-permute-start.21 = (bf16[4,128,2,128]{3,1,2,0:T(8,128)(2,1)}, bf16[4,128,2,128]{3,1,2,0:T(8,128)(2,1)S(1)}, u32[]{:S(2)}, u32[]{:S(2)}) collective-permute-start(bf16[4,128,2,128]{3,1,2,0:T(8,128)(2,1)} %get-tuple-element.26), channel_id=1, source_target_pairs={{0,56},{8,64},{16,72},{24,80},{32,88},{40,96},{48,104},{56,112},{6... | collective-permute-start | bytes 786440 | tf_op jit(solution)/shard_map/ppermute | solution.py:157
  69.0 15.7 %collective-permute-start.22 = (bf16[4,128,2,128]{3,1,2,0:T(8,128)(2,1)}, bf16[4,128,2,128]{3,1,2,0:T(8,128)(2,1)S(1)}, u32[]{:S(2)}, u32[]{:S(2)}) collective-permute-start(bf16[4,128,2,128]{3,1,2,0:T(8,128)(2,1)} %get-tuple-element.25), channel_id=1, source_target_pairs={{0,64},{8,72},{16,80},{24,88},{32,96},{40,104},{48,112},{56,120},{... | collective-permute-start | bytes 786440 | tf_op jit(solution)/shard_map/ppermute | solution.py:157
  72.1 20.0 %collective-permute-start.23 = (bf16[4,128,2,128]{3,1,2,0:T(8,128)(2,1)}, bf16[4,128,2,128]{3,1,2,0:T(8,128)(2,1)S(1)}, u32[]{:S(2)}, u32[]{:S(2)}) collective-permute-start(bf16[4,128,2,128]{3,1,2,0:T(8,128)(2,1)} %get-tuple-element.24), channel_id=1, source_target_pairs={{0,72},{8,80},{16,88},{24,96},{32,104},{40,112},{48,120},{56,0},{6... | collective-permute-start | bytes 786440 | tf_op jit(solution)/shard_map/ppermute | solution.py:157
  77.8 57.4 %copy-start.2 = (bf16[256,5120]{1,0:T(8,128)(2,1)S(1)}, bf16[256,5120]{1,0:T(8,128)(2,1)}, u32[]{:S(2)}) copy-start(bf16[256,5120]{1,0:T(8,128)(2,1)} %copy.84) | copy-start | bytes 7864324
  77.8 20.7 %collective-permute-start.24 = (bf16[4,128,2,128]{3,1,2,0:T(8,128)(2,1)}, bf16[4,128,2,128]{3,1,2,0:T(8,128)(2,1)S(1)}, u32[]{:S(2)}, u32[]{:S(2)}) collective-permute-start(bf16[4,128,2,128]{3,1,2,0:T(8,128)(2,1)} %get-tuple-element.23), channel_id=1, source_target_pairs={{0,80},{8,88},{16,96},{24,104},{32,112},{40,120},{48,0},{56,8},{64... | collective-permute-start | bytes 786440 | tf_op jit(solution)/shard_map/ppermute | solution.py:157
  80.8 31.2 %collective-permute-start.25 = (bf16[4,128,2,128]{3,1,2,0:T(8,128)(2,1)}, bf16[4,128,2,128]{3,1,2,0:T(8,128)(2,1)S(1)}, u32[]{:S(2)}, u32[]{:S(2)}) collective-permute-start(bf16[4,128,2,128]{3,1,2,0:T(8,128)(2,1)} %get-tuple-element.22), channel_id=1, source_target_pairs={{0,88},{8,96},{16,104},{24,112},{32,120},{40,0},{48,8},{56,16},{64... | collective-permute-start | bytes 786440 | tf_op jit(solution)/shard_map/ppermute | solution.py:157
  81.9 32.1 %collective-permute-start.26 = (bf16[4,128,2,128]{3,1,2,0:T(8,128)(2,1)}, bf16[4,128,2,128]{3,1,2,0:T(8,128)(2,1)S(1)}, u32[]{:S(2)}, u32[]{:S(2)}) collective-permute-start(bf16[4,128,2,128]{3,1,2,0:T(8,128)(2,1)} %get-tuple-element.21), channel_id=1, source_target_pairs={{0,96},{8,104},{16,112},{24,120},{32,0},{40,8},{48,16},{56,24},{64... | collective-permute-start | bytes 786440 | tf_op jit(solution)/shard_map/ppermute | solution.py:157
  84.7 30.3 %collective-permute-start.27 = (bf16[4,128,2,128]{3,1,2,0:T(8,128)(2,1)S(1)}, bf16[4,128,2,128]{3,1,2,0:T(8,128)(2,1)S(1)}, u32[]{:S(2)}, u32[]{:S(2)}) collective-permute-start(bf16[4,128,2,128]{3,1,2,0:T(8,128)(2,1)S(1)} %get-tuple-element.20), channel_id=1, source_target_pairs={{0,104},{8,112},{16,120},{24,0},{32,8},{40,16},{48,24},{56,32},{64... | collective-permute-start | bytes 786440 | tf_op jit(solution)/shard_map/ppermute | solution.py:157
  92.1 38.7 %collective-permute-start.28 = (bf16[4,128,2,128]{3,1,2,0:T(8,128)(2,1)S(1)}, bf16[4,128,2,128]{3,1,2,0:T(8,128)(2,1)S(1)}, u32[]{:S(2)}, u32[]{:S(2)}) collective-permute-start(bf16[4,128,2,128]{3,1,2,0:T(8,128)(2,1)S(1)} %get-tuple-element.19), channel_id=1, source_target_pairs={{0,112},{8,120},{16,0},{24,8},{32,16},{40,24},{48,32},{56,40},{64,... | collective-permute-start | bytes 786440 | tf_op jit(solution)/shard_map/ppermute | solution.py:157
  98.5 33.4 %collective-permute-start.29 = (bf16[4,128,2,128]{3,1,2,0:T(8,128)(2,1)S(1)}, bf16[4,128,2,128]{3,1,2,0:T(8,128)(2,1)S(1)}, u32[]{:S(2)}, u32[]{:S(2)}) collective-permute-start(bf16[4,128,2,128]{3,1,2,0:T(8,128)(2,1)S(1)} %get-tuple-element.18), channel_id=1, source_target_pairs={{0,120},{8,0},{16,8},{24,16},{32,24},{40,32},{48,40},{56,48},{64,5... | collective-permute-start | bytes 786440 | tf_op jit(solution)/shard_map/ppermute | solution.py:157
  135.2 10.2 %copy-start.1 = (bf16[256,5120]{1,0:T(8,128)(2,1)S(1)}, bf16[256,5120]{1,0:T(8,128)(2,1)}, u32[]{:S(2)}) copy-start(bf16[256,5120]{1,0:T(8,128)(2,1)} %all-gather.3.cloned.1.call-done) | copy-start | bytes 7864324
  135.2 10.2 %copy-start.4 = (f32[5120]{0:T(1024)S(1)}, f32[5120]{0:T(1024)}, u32[]{:S(2)}) copy-start(f32[5120]{0:T(1024)} %param.10) | copy-start | bytes 61444
  138.9 12.7 %collective-permute-start = (bf16[256,256]{1,0:T(8,128)(2,1)S(1)}, bf16[256,256]{1,0:T(8,128)(2,1)}, u32[]{:S(2)}, u32[]{:S(2)}) collective-permute-start(bf16[256,256]{1,0:T(8,128)(2,1)S(1)} %get-tuple-element.17), channel_id=1, source_target_pairs={{0,8},{8,16},{16,24},{24,32},{32,40},{40,48},{48,56},{56,64},{64,7... | collective-permute-start | bytes 393224 | tf_op jit(solution)/shard_map/ppermute | solution.py:213
  140.2 13.6 %collective-permute-start.1 = (bf16[256,256]{1,0:T(8,128)(2,1)S(1)}, bf16[256,256]{1,0:T(8,128)(2,1)S(1)}, u32[]{:S(2)}, u32[]{:S(2)}) collective-permute-start(bf16[256,256]{1,0:T(8,128)(2,1)S(1)} %get-tuple-element.17), channel_id=1, source_target_pairs={{0,16},{8,24},{16,32},{24,40},{32,48},{40,56},{48,64},{56,72},{64,... | collective-permute-start | bytes 393224 | tf_op jit(solution)/shard_map/ppermute | solution.py:213
  141.5 13.6 %collective-permute-start.2 = (bf16[256,256]{1,0:T(8,128)(2,1)S(1)}, bf16[256,256]{1,0:T(8,128)(2,1)S(1)}, u32[]{:S(2)}, u32[]{:S(2)}) collective-permute-start(bf16[256,256]{1,0:T(8,128)(2,1)S(1)} %get-tuple-element.17), channel_id=1, source_target_pairs={{0,24},{8,32},{16,40},{24,48},{32,56},{40,64},{48,72},{56,80},{64,... | collective-permute-start | bytes 393224 | tf_op jit(solution)/shard_map/ppermute | solution.py:213
  142.8 13.6 %collective-permute-start.3 = (bf16[256,256]{1,0:T(8,128)(2,1)S(1)}, bf16[256,256]{1,0:T(8,128)(2,1)S(1)}, u32[]{:S(2)}, u32[]{:S(2)}) collective-permute-start(bf16[256,256]{1,0:T(8,128)(2,1)S(1)} %get-tuple-element.17), channel_id=1, source_target_pairs={{0,32},{8,40},{16,48},{24,56},{32,64},{40,72},{48,80},{56,88},{64,... | collective-permute-start | bytes 393224 | tf_op jit(solution)/shard_map/ppermute | solution.py:213
  144.1 17.9 %collective-permute-start.4 = (bf16[256,256]{1,0:T(8,128)(2,1)S(1)}, bf16[256,256]{1,0:T(8,128)(2,1)S(1)}, u32[]{:S(2)}, u32[]{:S(2)}) collective-permute-start(bf16[256,256]{1,0:T(8,128)(2,1)S(1)} %get-tuple-element.17), channel_id=1, source_target_pairs={{0,40},{8,48},{16,56},{24,64},{32,72},{40,80},{48,88},{56,96},{64,... | collective-permute-start | bytes 393224 | tf_op jit(solution)/shard_map/ppermute | solution.py:213
  151.6 13.3 %collective-permute-start.5 = (bf16[256,256]{1,0:T(8,128)(2,1)S(1)}, bf16[256,256]{1,0:T(8,128)(2,1)S(1)}, u32[]{:S(2)}, u32[]{:S(2)}) collective-permute-start(bf16[256,256]{1,0:T(8,128)(2,1)S(1)} %get-tuple-element.17), channel_id=1, source_target_pairs={{0,48},{8,56},{16,64},{24,72},{32,80},{40,88},{48,96},{56,104},{64... | collective-permute-start | bytes 393224 | tf_op jit(solution)/shard_map/ppermute | solution.py:213
  153.8 13.7 %collective-permute-start.6 = (bf16[256,256]{1,0:T(8,128)(2,1)S(1)}, bf16[256,256]{1,0:T(8,128)(2,1)S(1)}, u32[]{:S(2)}, u32[]{:S(2)}) collective-permute-start(bf16[256,256]{1,0:T(8,128)(2,1)S(1)} %get-tuple-element.17), channel_id=1, source_target_pairs={{0,56},{8,64},{16,72},{24,80},{32,88},{40,96},{48,104},{56,112},{6... | collective-permute-start | bytes 393224 | tf_op jit(solution)/shard_map/ppermute | solution.py:213
  155.2 16.9 %collective-permute-start.7 = (bf16[256,256]{1,0:T(8,128)(2,1)S(1)}, bf16[256,256]{1,0:T(8,128)(2,1)S(1)}, u32[]{:S(2)}, u32[]{:S(2)}) collective-permute-start(bf16[256,256]{1,0:T(8,128)(2,1)S(1)} %get-tuple-element.17), channel_id=1, source_target_pairs={{0,64},{8,72},{16,80},{24,88},{32,96},{40,104},{48,112},{56,120},{... | collective-permute-start | bytes 393224 | tf_op jit(solution)/shard_map/ppermute | solution.py:213
  156.5 16.9 %collective-permute-start.8 = (bf16[256,256]{1,0:T(8,128)(2,1)S(1)}, bf16[256,256]{1,0:T(8,128)(2,1)S(1)}, u32[]{:S(2)}, u32[]{:S(2)}) collective-permute-start(bf16[256,256]{1,0:T(8,128)(2,1)S(1)} %get-tuple-element.17), channel_id=1, source_target_pairs={{0,72},{8,80},{16,88},{24,96},{32,104},{40,112},{48,120},{1,73},{9... | collective-permute-start | bytes 393224 | tf_op jit(solution)/shard_map/ppermute | solution.py:213
  162.1 14.1 %collective-permute-start.9 = (bf16[256,256]{1,0:T(8,128)(2,1)S(1)}, bf16[256,256]{1,0:T(8,128)(2,1)S(1)}, u32[]{:S(2)}, u32[]{:S(2)}) collective-permute-start(bf16[256,256]{1,0:T(8,128)(2,1)S(1)} %get-tuple-element.17), channel_id=1, source_target_pairs={{0,80},{8,88},{16,96},{24,104},{32,112},{40,120},{1,81},{9,89},{17... | collective-permute-start | bytes 393224 | tf_op jit(solution)/shard_map/ppermute | solution.py:213
  164.9 13.6 %collective-permute-start.10 = (bf16[256,256]{1,0:T(8,128)(2,1)S(1)}, bf16[256,256]{1,0:T(8,128)(2,1)S(1)}, u32[]{:S(2)}, u32[]{:S(2)}) collective-permute-start(bf16[256,256]{1,0:T(8,128)(2,1)S(1)} %get-tuple-element.17), channel_id=1, source_target_pairs={{0,88},{8,96},{16,104},{24,112},{32,120},{1,89},{9,97},{17,105},{2... | collective-permute-start | bytes 393224 | tf_op jit(solution)/shard_map/ppermute | solution.py:213
  167.5 17.0 %collective-permute-start.11 = (bf16[256,256]{1,0:T(8,128)(2,1)S(1)}, bf16[256,256]{1,0:T(8,128)(2,1)S(1)}, u32[]{:S(2)}, u32[]{:S(2)}) collective-permute-start(bf16[256,256]{1,0:T(8,128)(2,1)S(1)} %get-tuple-element.17), channel_id=1, source_target_pairs={{0,96},{8,104},{16,112},{24,120},{1,97},{9,105},{17,113},{25,121},... | collective-permute-start | bytes 393224 | tf_op jit(solution)/shard_map/ppermute | solution.py:213
  172.1 12.6 %collective-permute-start.12 = (bf16[256,256]{1,0:T(8,128)(2,1)S(1)}, bf16[256,256]{1,0:T(8,128)(2,1)S(1)}, u32[]{:S(2)}, u32[]{:S(2)}) collective-permute-start(bf16[256,256]{1,0:T(8,128)(2,1)S(1)} %get-tuple-element.17), channel_id=1, source_target_pairs={{0,104},{8,112},{16,120},{1,105},{9,113},{17,121},{2,106},{10,114}... | collective-permute-start | bytes 393224 | tf_op jit(solution)/shard_map/ppermute | solution.py:213
  173.4 16.1 %collective-permute-start.13 = (bf16[256,256]{1,0:T(8,128)(2,1)S(1)}, bf16[256,256]{1,0:T(8,128)(2,1)S(1)}, u32[]{:S(2)}, u32[]{:S(2)}) collective-permute-start(bf16[256,256]{1,0:T(8,128)(2,1)S(1)} %get-tuple-element.17), channel_id=1, source_target_pairs={{0,112},{8,120},{1,113},{9,121},{2,114},{10,122},{3,115},{11,123},... | collective-permute-start | bytes 393224 | tf_op jit(solution)/shard_map/ppermute | solution.py:213
  176.2 13.5 %collective-permute-start.14 = (bf16[256,256]{1,0:T(8,128)(2,1)S(1)}, bf16[256,256]{1,0:T(8,128)(2,1)S(1)}, u32[]{:S(2)}, u32[]{:S(2)}) collective-permute-start(bf16[256,256]{1,0:T(8,128)(2,1)S(1)} %get-tuple-element.17), channel_id=1, source_target_pairs={{0,120},{1,121},{2,122},{3,123},{4,124},{5,125},{6,126},{7,127}} | collective-permute-start | bytes 393224 | tf_op jit(solution)/shard_map/ppermute | solution.py:213
  189.7 29.9 %copy-start.3 = (bf16[4096,256]{1,0:T(8,128)(2,1)}, bf16[4096,256]{1,0:T(8,128)(2,1)S(1)}, u32[]{:S(2)}) copy-start(bf16[4096,256]{1,0:T(8,128)(2,1)S(1)} %constant_dynamic-update-slice_fusion.kv_ref) | copy-start | bytes 6291460
  283.7 21.9 %collective-permute-start.36 = (bf16[256,640]{1,0:T(8,128)(2,1)S(1)}, bf16[256,640]{1,0:T(8,128)(2,1)S(1)}, u32[]{:S(2)}, u32[]{:S(2)}) collective-permute-start(bf16[256,640]{1,0:T(8,128)(2,1)S(1)} %get-tuple-element.35), channel_id=1, source_target_pairs={{0,7},{1,0},{2,1},{3,2},{4,3},{5,4},{6,5},{7,6},{8,15},{9,8},{10,9... | collective-permute-start | bytes 983048 | tf_op jit(solution)/shard_map/ppermute | solution.py:241
  287.3 18.3 %collective-permute-start.35 = (bf16[256,640]{1,0:T(8,128)(2,1)S(1)}, bf16[256,640]{1,0:T(8,128)(2,1)S(1)}, u32[]{:S(2)}, u32[]{:S(2)}) collective-permute-start(bf16[256,640]{1,0:T(8,128)(2,1)S(1)} %get-tuple-element.36), channel_id=1, source_target_pairs={{0,6},{1,7},{2,0},{3,1},{4,2},{5,3},{6,4},{7,5},{8,14},{9,15},{10,... | collective-permute-start | bytes 983048 | tf_op jit(solution)/shard_map/ppermute | solution.py:241
  287.3 22.2 %collective-permute-start.34 = (bf16[256,640]{1,0:T(8,128)(2,1)S(1)}, bf16[256,640]{1,0:T(8,128)(2,1)S(1)}, u32[]{:S(2)}, u32[]{:S(2)}) collective-permute-start(bf16[256,640]{1,0:T(8,128)(2,1)S(1)} %get-tuple-element.37), channel_id=1, source_target_pairs={{0,5},{1,6},{2,7},{3,0},{4,1},{5,2},{6,3},{7,4},{8,13},{9,14},{10,... | collective-permute-start | bytes 983048 | tf_op jit(solution)/shard_map/ppermute | solution.py:241
  289.0 20.5 %collective-permute-start.33 = (bf16[256,640]{1,0:T(8,128)(2,1)S(1)}, bf16[256,640]{1,0:T(8,128)(2,1)S(1)}, u32[]{:S(2)}, u32[]{:S(2)}) collective-permute-start(bf16[256,640]{1,0:T(8,128)(2,1)S(1)} %get-tuple-element.38), channel_id=1, source_target_pairs={{0,4},{1,5},{2,6},{3,7},{4,0},{5,1},{6,2},{7,3},{8,12},{9,13},{10,... | collective-permute-start | bytes 983048 | tf_op jit(solution)/shard_map/ppermute | solution.py:241
  289.1 24.8 %collective-permute-start.32 = (bf16[256,640]{1,0:T(8,128)(2,1)S(1)}, bf16[256,640]{1,0:T(8,128)(2,1)S(1)}, u32[]{:S(2)}, u32[]{:S(2)}) collective-permute-start(bf16[256,640]{1,0:T(8,128)(2,1)S(1)} %get-tuple-element.39), channel_id=1, source_target_pairs={{0,3},{1,4},{2,5},{3,6},{4,7},{5,0},{6,1},{7,2},{8,11},{9,12},{10,... | collective-permute-start | bytes 983048 | tf_op jit(solution)/shard_map/ppermute | solution.py:241
  305.6 9.0 %collective-permute-start.31 = (bf16[256,640]{1,0:T(8,128)(2,1)S(1)}, bf16[256,640]{1,0:T(8,128)(2,1)}, u32[]{:S(2)}, u32[]{:S(2)}) collective-permute-start(bf16[256,640]{1,0:T(8,128)(2,1)S(1)} %get-tuple-element.40), channel_id=1, source_target_pairs={{0,2},{1,3},{2,4},{3,5},{4,6},{5,7},{6,0},{7,1},{8,10},{9,11},{10,... | collective-permute-start | bytes 983048 | tf_op jit(solution)/shard_map/ppermute | solution.py:241
  305.6 12.4 %collective-permute-start.30 = (bf16[256,640]{1,0:T(8,128)(2,1)S(1)}, bf16[256,640]{1,0:T(8,128)(2,1)}, u32[]{:S(2)}, u32[]{:S(2)}) collective-permute-start(bf16[256,640]{1,0:T(8,128)(2,1)S(1)} %get-tuple-element.34), channel_id=1, source_target_pairs={{0,1},{1,2},{2,3},{3,4},{4,5},{5,6},{6,7},{7,0},{8,9},{9,10},{10,1... | collective-permute-start | bytes 983048 | tf_op jit(solution)/shard_map/ppermute | solution.py:241
Sparse Core Ops, SparseCore 0:
  9.6 51.6 all-gather.2
  63.7 99.8 all-gather.4
